TPU v7x, 256 devices: a whole 4x4x8 slice. The times are simulated.
256 devices in a mesh: rows: 16 (over z, y_hi), bx: 4 (over y_lo, core), by: 4 (over x).
Axes of the slice: x: 4, y: 4 (y_hi: 2, y_lo: 2; y = y_hi * 2 + y_lo), z: 8, core: 2. Of those that a mesh axis runs over, the one named last changes fastest.
Arguments:
- pair_mult: bfloat16 [1048576, 256], P(('rows', 'bx', 'by')), may hold values from -1.5 to 1.5
- pair_dens: float32 [1048576], P(('rows', 'bx', 'by')), may hold values from -3 to 3
- pair_live: int32 [1048576], P(('rows', 'bx', 'by')), may hold values 0 or 1
- pair_box: int32 [1048576], P(('rows', 'bx', 'by')), may hold values from 0 to 767
- inter_mask: int32 [128, 32, 32, 98], P('rows', 'bx', 'by'), may hold values 0 or 1
- row_scale: float32 [98, 256], replicated, may hold values from 0.3 to 1.5
- col_scale: float32 [98, 256], replicated, may hold values from 0.3 to 1.5
- base: bfloat16 [256, 256], replicated, may hold values from -0.0390625 to 0.0390625
- lattice: float32 [256, 256], replicated, may hold values from -0.0009765625 to 0.0009765625
Outputs:
- box_locals: bfloat16 [128, 32, 32, 256], P('rows', 'bx', 'by')
- pair_j: float32 [1048576], P(('rows', 'bx', 'by'))
Inputs may be any that keep to these rules, and one draw needn't show every extreme that they name: `pair_box`: numbers a box of the pair's own x, y slab as (l * 8 + x) * 8 + y with l in 0..11, x in 0..7, y in 0..7, where level l is the box z = (rows index of the device * 8 + l - 2) mod 128.
All inputs are finite; a program needn't handle non-finite values. No bound on the sum of `pair_live` or of `inter_mask` on one device may be relied on, other than what follows from the above.
Results may differ from a plain program's by a relative error of at most 0.007.
Values may be sent and summed in bfloat16 or wider, within the bound.
No kernel may reach another device: no remote copies, remote signals or barrier semaphores. Data moves between devices by JAX's collectives and lax.ppermute only.
A program may use at most 128 MiB of HBM per device.

v0:
```python
import numpy as np
import jax
import jax.numpy as jnp
from jax import lax
from jax.experimental import pallas as pl
from jax.experimental.pallas import tpu as pltpu
from jax.sharding import PartitionSpec as P


def padded_2(x, sides, width):
    for axis, dim in sides:
        count, length = (lax.axis_size(axis), x.shape[dim])
        up = [(i, (i + 1) % count) for i in range(count)]
        down = [(j, i) for i, j in up]
        last = lax.slice_in_dim(x, length - width, length, axis=dim)
        leading = lax.slice_in_dim(x, 0, width, axis=dim)
        before = lax.ppermute(last, axis, up)
        after = lax.ppermute(leading, axis, down)
        x = jnp.concatenate([before, x, after], axis=dim)
    return x


def offset_table():
    listed = []
    for shift_z in range(-2, 3):
        for shift_x in range(-2, 3):
            for shift_y in range(-2, 3):
                if max(abs(shift_z), abs(shift_x), abs(shift_y)) == 2:
                    listed.append((shift_z, shift_x, shift_y))
    return listed


def axis_sum(x, axis):
    count = lax.axis_size(axis)
    stride = 1
    while stride < count:
        group = min(4, count // stride)
        span = stride * group
        total = x
        for k in range(1, group):
            pairs = []
            for i in range(count):
                block, rest = divmod(i, span)
                pairs.append((i, block * span + (rest + k * stride) % span))
            total = total + lax.ppermute(x, axis, pairs)
        x = total
        stride = span
    return x


def far_kernel(tab_ref, ysh_ref, mask_ref, rs_ref, cs_ref, base_ref, lat_ref, out_ref, acc_ref):
    rows = acc_ref.shape[0]
    lanes = mask_ref.shape[1]
    acc_ref[...] = jnp.zeros(acc_ref.shape, jnp.float32)
    lane = lax.broadcasted_iota(jnp.int32, (rows, lanes), 1)

    def body(o, carry):
        a = tab_ref[3 * o]
        b = tab_ref[3 * o + 1]
        c = tab_ref[3 * o + 2]
        win = ysh_ref[c, pl.ds(a, 8), pl.ds(b, 8), :, :].reshape(rows, -1)
        gate = jnp.sum(jnp.where(lane == o, mask_ref[...], 0.0), axis=1, keepdims=True)
        scaled = (win * gate * rs_ref[pl.ds(o, 1), :]).astype(jnp.bfloat16)
        product = jnp.dot(scaled, base_ref[...], preferred_element_type=jnp.float32)
        acc_ref[...] += product * cs_ref[pl.ds(o, 1), :]
        return carry

    lax.fori_loop(0, tab_ref.shape[0] // 3, body, 0)
    out_ref[...] = (acc_ref[...] + lat_ref[...]).astype(out_ref.dtype)


def far_field(ysh, masks, row_scale, col_scale, base, lattice_term):
    rows = masks.shape[0]
    components = base.shape[1]
    table = np.array([[a + 2, b + 2, c + 2] for a, b, c in offset_table()], np.int32).reshape(-1)
    vmem = pltpu.MemorySpace.VMEM if hasattr(pltpu, "MemorySpace") else pltpu.VMEM
    smem = pltpu.MemorySpace.SMEM if hasattr(pltpu, "MemorySpace") else pltpu.SMEM
    return pl.pallas_call(
        far_kernel,
        out_shape=jax.ShapeDtypeStruct((rows, components), jnp.bfloat16),
        in_specs=[pl.BlockSpec(memory_space=smem)] + [pl.BlockSpec(memory_space=vmem)] * 6,
        out_specs=pl.BlockSpec(memory_space=vmem),
        scratch_shapes=[pltpu.VMEM((rows, components), jnp.float32)],
        compiler_params=pltpu.CompilerParams(vmem_limit_bytes=48 * 1024 * 1024),
    )(jnp.asarray(table), ysh, masks, row_scale, col_scale, base, lattice_term.reshape(1, components))


def per_device(
    pair_mult, pair_dens, pair_live, pair_box, inter_mask, row_scale, col_scale, base, lattice
):
    components = pair_mult.shape[1]
    depth, width_x, width_y, offsets = inter_mask.shape
    near_boxes = (depth + 4) * width_x * width_y
    weighted = (
        (pair_dens * pair_live.astype(jnp.float32))[:, None] * pair_mult.astype(jnp.float32)
    ).astype(jnp.bfloat16)
    cell_part = jnp.sum(weighted.astype(jnp.float32), 0)
    cell = axis_sum(axis_sum(axis_sum(cell_part, "by"), "bx"), "rows")
    lattice_term = jnp.dot(cell, lattice, precision=lax.Precision.HIGHEST)
    labels = lax.iota(jnp.int32, near_boxes)
    selector = (labels[:, None] == pair_box[None, :]).astype(jnp.bfloat16)
    partial_near = jnp.dot(selector, weighted, preferred_element_type=jnp.float32)
    partial_near = partial_near.reshape(depth + 4, width_x, width_y, components)
    bordered = padded_2(partial_near, (("rows", 0),), 2)
    stored = partial_near[2 : 2 + depth]
    stored = stored.at[:2].add(bordered[:2])
    stored = stored.at[depth - 2 :].add(bordered[depth + 6 :])
    padded = padded_2(stored, (("rows", 0), ("bx", 1), ("by", 2)), 2)
    ysh = jnp.stack([padded[:, :, c : c + width_y] for c in range(5)])
    masks = inter_mask.reshape(depth * width_x * width_y, offsets).astype(jnp.float32)
    far = far_field(ysh, masks, row_scale, col_scale, base, lattice_term)
    box_locals = far.reshape(depth, width_x, width_y, components)
    near_locals = padded_2(box_locals, (("rows", 0),), 2)
    flat_locals = near_locals.reshape(near_boxes, components)
    onehot = (pair_box[:, None] == labels[None, :]).astype(jnp.bfloat16)
    picked_rows = jnp.dot(onehot, flat_locals, preferred_element_type=jnp.float32)
    pair_j = jnp.sum(pair_mult.astype(jnp.float32) * picked_rows, -1)
    return (box_locals, pair_j)


def solution(mesh):
    return jax.shard_map(
        per_device,
        mesh=mesh,
        in_specs=(
            P(("rows", "bx", "by"), None),
            P(("rows", "bx", "by")),
            P(("rows", "bx", "by")),
            P(("rows", "bx", "by")),
            P("rows", "bx", "by", None),
            P(),
            P(),
            P(),
            P(),
        ),
        out_specs=(P("rows", "bx", "by", None), P(("rows", "bx", "by"))),
        check_vma=False,
    )
```

profile of v0, /device:TPU:6, one launch (start us, length us, event | category | flops | bytes accessed | tf_op | source)
XLA Modules:
  0.0 107.9 jit_solution(15587959268107840707)
XLA Ops:
  0.6 0.0 copy-start
  0.7 3.0 %copy.12 = bf16[4096,256]{0,1:T(8,128)(2,1)S(1)} copy(bf16[4096,256]{1,0:T(8,128)(2,1)} %param.14) | data formatting | bytes 4194304 | tf_op args[0]
  3.7 0.5 convert_reduce_fusion
  4.2 0.9 collective-permute-start.10
  5.1 2.4 %collective-permute-start.8 = (f32[256]{0:T(256)S(1)}, f32[256]{0:T(256)S(1)}, u32[]{:S(2)}, u32[]{:S(2)}) collective-permute-start(f32[256]{0:T(256)S(1)} %convert_reduce_fusion), channel_id=1, source_target_pairs={{0,1},{1,2},{2,3},{3,0},{4,5},{5,6},{6,7},{7,4},{8,9},{9,10},{10,1... | collective-permute-start | bytes 3080 | tf_op jit(solution)/shard_map/ppermute | solution.py:45
  7.5 0.4 collective-permute-start.9
  7.9 2.4 %fusion = f32[768,256]{1,0:T(8,128)S(1)} fusion(s32[4096]{0:T(1024)S(1)} %copy-done.9, bf16[4096,256]{0,1:T(8,128)(2,1)S(1)} %copy.12, f32[4096]{0:T(1024)S(1)} %convert_multiply_fusion.1), kind=kOutput, calls=%fused_computation.2 | convolution fusion | flops 1616904192 | bytes 2916352 | tf_op jit(solution)/shard_map/dot_general | solution.py:102
  10.3 3.1 %collective-permute-start = (f32[2,8,8,256]{3,2,1,0:T(8,128)S(1)}, f32[2,8,8,256]{3,2,1,0:T(8,128)S(1)}, u32[]{:S(2)}, u32[]{:S(2)}) collective-permute-start(f32[2,8,8,256]{3,2,1,0:T(8,128)S(1)} %bitcast.39), channel_id=1, source_target_pairs={{0,16},{16,32},{32,48},{48,64},{64,80},{80,96},{96,112},{112,128},... | collective-permute-start | bytes 393224 | tf_op jit(solution)/shard_map/ppermute | solution.py:17
  13.4 5.4 %collective-permute-start.1 = (f32[2,8,8,256]{3,2,1,0:T(8,128)S(1)}, f32[2,8,8,256]{3,2,1,0:T(8,128)S(1)}, u32[]{:S(2)}, u32[]{:S(2)}) collective-permute-start(f32[2,8,8,256]{3,2,1,0:T(8,128)S(1)} %bitcast.38), channel_id=1, source_target_pairs={{16,0},{32,16},{48,32},{64,48},{80,64},{96,80},{112,96},{128,112},... | collective-permute-start | bytes 393224 | tf_op jit(solution)/shard_map/ppermute | solution.py:18
  18.8 0.0 collective-permute-done.10
  18.9 0.0 collective-permute-done.8
  18.9 0.0 collective-permute-done.9
  18.9 0.1 collective-permute-start.11
  19.0 0.8 collective-permute-start.12
  19.7 1.4 %collective-permute-start.13 = (f32[256]{0:T(256)S(1)}, f32[256]{0:T(256)S(1)}, u32[]{:S(2)}, u32[]{:S(2)}) collective-permute-start(f32[256]{0:T(256)S(1)} %add_add_fusion.3), channel_id=1, source_target_pairs={{0,12},{4,0},{8,4},{12,8},{1,13},{5,1},{9,5},{13,9},{2,14},{6,2},{... | collective-permute-start | bytes 3080 | tf_op jit(solution)/shard_map/ppermute | solution.py:45
  21.1 0.5 collective-permute-done
  21.6 1.0 collective-permute-done.1
  22.8 5.4 %collective-permute-start.3 = (f32[2,8,8,256]{3,2,1,0:T(8,128)S(1)}, f32[2,8,8,256]{3,2,1,0:T(8,128)S(1)}, u32[]{:S(2)}, u32[]{:S(2)}) collective-permute-start(f32[2,8,8,256]{3,2,1,0:T(8,128)S(1)} %slice.148), channel_id=1, source_target_pairs={{16,0},{32,16},{48,32},{64,48},{80,64},{96,80},{112,96},{128,112},... | collective-permute-start | bytes 393224 | tf_op jit(solution)/shard_map/ppermute | solution.py:18
  28.2 0.0 collective-permute-start.2
  28.2 0.0 collective-permute-done.11
  28.2 0.0 collective-permute-done.12
  28.2 0.0 collective-permute-done.13
  28.2 0.1 collective-permute-start.14
  28.3 1.0 collective-permute-start.15
  29.3 3.4 %collective-permute-start.16 = (f32[256]{0:T(256)S(1)}, f32[256]{0:T(256)S(1)}, u32[]{:S(2)}, u32[]{:S(2)}) collective-permute-start(f32[256]{0:T(256)S(1)} %add_add_fusion.2), channel_id=1, source_target_pairs={{0,48},{16,0},{32,16},{48,32},{64,112},{80,64},{96,80},{112,96},{1... | collective-permute-start | bytes 3080 | tf_op jit(solution)/shard_map/ppermute | solution.py:45
  32.7 0.0 collective-permute-done.3
  32.7 4.0 %collective-permute-done.2 = f32[2,8,8,256]{3,2,1,0:T(8,128)S(1)} collective-permute-done((f32[2,8,8,256]{3,2,1,0:T(8,128)S(1)}, f32[2,8,8,256]{3,2,1,0:T(8,128)S(1)}, u32[]{:S(2)}, u32[]{:S(2)}) %collective-permute-start.2) | collective-permute-done | bytes 131104 | tf_op jit(solution)/shard_map/ppermute | solution.py:17
  36.8 0.1 collective-permute-start.4
  36.9 1.7 %collective-permute-start.5 = (f32[12,2,8,256]{3,2,1,0:T(8,128)S(1)}, f32[12,2,8,256]{3,2,1,0:T(8,128)S(1)}, u32[]{:S(2)}, u32[]{:S(2)}) collective-permute-start(f32[12,2,8,256]{3,2,1,0:T(8,128)S(1)} %get-tuple-element.33), channel_id=1, source_target_pairs={{4,0},{8,4},{12,8},{0,12},{5,1},{9,5},{13,9},{1,13},{6,2},{10,6},{... | collective-permute-start | bytes 589832 | tf_op jit(solution)/shard_map/ppermute | solution.py:18
  38.6 0.0 collective-permute-done.14
  38.6 0.0 collective-permute-done.15
  38.6 0.0 collective-permute-done.16
  38.6 2.4 %collective-permute-start.17 = (f32[256]{0:T(256)S(1)}, f32[256]{0:T(256)S(1)}, u32[]{:S(2)}, u32[]{:S(2)}) collective-permute-start(f32[256]{0:T(256)S(1)} %add_add_fusion.1), channel_id=1, source_target_pairs={{0,64},{16,80},{32,96},{48,112},{64,128},{80,144},{96,160},{112,17... | collective-permute-start | bytes 3080 | tf_op jit(solution)/shard_map/ppermute | solution.py:45
  41.0 2.3 %collective-permute-start.18 = (f32[256]{0:T(256)S(1)}, f32[256]{0:T(256)S(1)}, u32[]{:S(2)}, u32[]{:S(2)}) collective-permute-start(f32[256]{0:T(256)S(1)} %add_add_fusion.1), channel_id=1, source_target_pairs={{0,128},{16,144},{32,160},{48,176},{64,192},{80,208},{96,224},{112... | collective-permute-start | bytes 3080 | tf_op jit(solution)/shard_map/ppermute | solution.py:45
  43.4 3.1 %collective-permute-start.19 = (f32[256]{0:T(256)S(1)}, f32[256]{0:T(256)S(1)}, u32[]{:S(2)}, u32[]{:S(2)}) collective-permute-start(f32[256]{0:T(256)S(1)} %add_add_fusion.1), channel_id=1, source_target_pairs={{0,192},{16,208},{32,224},{48,240},{64,0},{80,16},{96,32},{112,48}... | collective-permute-start | bytes 3080 | tf_op jit(solution)/shard_map/ppermute | solution.py:45
  46.4 0.0 collective-permute-done.4
  46.4 0.0 collective-permute-done.5
  46.5 0.1 pad_maximum_fusion.1
  46.5 0.2 fusion.12
  46.7 2.2 %collective-permute-start.6 = (f32[12,12,2,256]{3,2,1,0:T(2,128)S(1)}, f32[12,12,2,256]{3,2,1,0:T(2,128)S(1)}, u32[]{:S(2)}, u32[]{:S(2)}) collective-permute-start(f32[12,12,2,256]{3,2,1,0:T(2,128)S(1)} %get-tuple-element.31), channel_id=1, source_target_pairs={{0,1},{1,2},{2,3},{3,0},{4,5},{5,6},{6,7},{7,4},{8,9},{9,10},{10,1... | collective-permute-start | bytes 884744 | tf_op jit(solution)/shard_map/ppermute | solution.py:17
  48.9 0.0 collective-permute-start.7
  48.9 0.0 collective-permute-done.17
  48.9 0.0 collective-permute-done.18
  48.9 0.2 fusion.15.lat_ref
  49.1 5.7 %collective-permute-done.6 = f32[12,12,2,256]{3,2,1,0:T(2,128)S(1)} collective-permute-done((f32[12,12,2,256]{3,2,1,0:T(2,128)S(1)}, f32[12,12,2,256]{3,2,1,0:T(2,128)S(1)}, u32[]{:S(2)}, u32[]{:S(2)}) %collective-permute-start.6) | collective-permute-done | bytes 294944 | tf_op jit(solution)/shard_map/ppermute | solution.py:17
  54.8 3.0 %collective-permute-done.7 = f32[12,12,2,256]{3,2,1,0:T(2,128)S(1)} collective-permute-done((f32[12,12,2,256]{3,2,1,0:T(2,128)S(1)}, f32[12,12,2,256]{3,2,1,0:T(2,128)S(1)}, u32[]{:S(2)}, u32[]{:S(2)}) %collective-permute-start.7) | collective-permute-done | bytes 294944 | tf_op jit(solution)/shard_map/ppermute | solution.py:18
  57.9 0.7 pad_maximum_fusion
  58.6 0.1 fusion.11
  58.7 0.2 fusion.10
  58.9 0.1 bitcast_dynamic-update-slice_fusion
  59.0 0.0 copy-start.1
  59.0 0.0 copy-start.2
  59.0 0.0 copy-start.3
  59.0 0.0 copy-start.4
  59.0 0.2 fusion.9
  59.2 0.2 fusion.8.ysh_ref
  59.3 2.5 %copy-done.5 = f32[5,12,12,8,256]{4,3,2,1,0:T(8,128)} copy-done((f32[5,12,12,8,256]{4,3,2,1,0:T(8,128)}, f32[5,12,12,8,256]{4,3,2,1,0:T(8,128)S(1)}, u32[]{:S(2)}) %copy-start.5) | copy-done | bytes 5898264
  61.9 31.9 %shard_map.113 = bf16[512,256]{1,0:T(8,128)(2,1)} custom-call(s32[294]{0:T(512)S(1)} %copy-done.4, f32[5,12,12,8,256]{4,3,2,1,0:T(8,128)} %copy-done.5, f32[512,98]{1,0:T(8,128)S(1)} %bitcast.32, f32[98,256]{1,0:T(8,128)S(1)} %copy-done.2, f32[98,256]{1,0:T(8,128)S(1)} %copy-done.3, bf16[256,256]{1,0:T(8,128)(2,1)S(1)} %copy-done.1, f32[1,256]{1,0:T(1,128)S(1)} %fusion.15.lat_ref), custom_call_target="tpu_custom_call" | custom-call | tf_op jit(solution)/shard_map/pallas_call | solution.py:78
  93.8 0.9 fusion.14
  94.7 0.1 collective-permute-start.20
  94.8 5.6 %collective-permute-start.21 = (bf16[2,8,8,256]{3,2,1,0:T(8,128)(2,1)S(1)}, bf16[2,8,8,256]{3,2,1,0:T(8,128)(2,1)S(1)}, u32[]{:S(2)}, u32[]{:S(2)}) collective-permute-start(bf16[2,8,8,256]{3,2,1,0:T(8,128)(2,1)S(1)} %bitcast.40), channel_id=1, source_target_pairs={{16,0},{32,16},{48,32},{64,48},{80,64},{96,80},{112,96},{128,112},... | collective-permute-start | bytes 196616 | tf_op jit(solution)/shard_map/ppermute | solution.py:18
  100.4 2.2 %collective-permute-done.20 = bf16[2,8,8,256]{3,2,1,0:T(8,128)(2,1)S(1)} collective-permute-done((bf16[2,8,8,256]{3,2,1,0:T(8,128)(2,1)S(1)}, bf16[2,8,8,256]{3,2,1,0:T(8,128)(2,1)S(1)}, u32[]{:S(2)}, u32[]{:S(2)}) %collective-permute-start.20) | collective-permute-done | bytes 65568 | tf_op jit(solution)/shard_map/ppermute | solution.py:17
  102.7 1.0 pad_maximum_fusion.2
  103.7 4.3 %fusion.7 = f32[4096]{0:T(1024)} fusion(bf16[768,256]{1,0:T(8,128)(2,1)S(1)} %bitcast.37, s32[4096]{0:T(1024)S(1)} %copy-done.9, bf16[4096,256]{0,1:T(8,128)(2,1)S(1)} %copy.12), kind=kOutput, calls=%fused_computation.12 | convolution fusion | flops 1616900096 | bytes 2523136 | tf_op jit(solution)/shard_map/dot_general | solution.py:116
  (28 shorter events, 0.3 us)
Async XLA Ops:
  0.6 48.3 %copy-start = (f32[256,256]{1,0:T(8,128)S(1)}, f32[256,256]{1,0:T(8,128)}, u32[]{:S(2)}) copy-start(f32[256,256]{1,0:T(8,128)} %param.22) | copy-start | bytes 786436
  0.6 3.0 %copy-start.7 = (f32[4096]{0:T(1024)S(1)}, f32[4096]{0:T(1024)}, u32[]{:S(2)}) copy-start(f32[4096]{0:T(1024)} %param.15) | copy-start | bytes 49156
  0.7 3.0 %copy-start.8 = (s32[4096]{0:T(1024)S(1)}, s32[4096]{0:T(1024)}, u32[]{:S(2)}) copy-start(s32[4096]{0:T(1024)} %param.16) | copy-start | bytes 49156
  0.7 7.2 %copy-start.9 = (s32[4096]{0:T(1024)S(1)}, s32[4096]{0:T(1024)}, u32[]{:S(2)}) copy-start(s32[4096]{0:T(1024)} %param.17) | copy-start | bytes 49156
  4.2 14.6 %copy-start.6 = (s32[8,8,8,98]{3,2,1,0:T(8,128)S(1)}, s32[8,8,8,98]{3,2,1,0:T(8,128)}, u32[]{:S(2)}) copy-start(s32[8,8,8,98]{3,2,1,0:T(8,128)} %param.18) | copy-start | bytes 602116
  4.2 14.7 %collective-permute-start.10 = (f32[256]{0:T(256)S(1)}, f32[256]{0:T(256)S(1)}, u32[]{:S(2)}, u32[]{:S(2)}) collective-permute-start(f32[256]{0:T(256)S(1)} %convert_reduce_fusion), channel_id=1, source_target_pairs={{0,3},{1,0},{2,1},{3,2},{4,7},{5,4},{6,5},{7,6},{8,11},{9,8},{10,9... | collective-permute-start | bytes 3080 | tf_op jit(solution)/shard_map/ppermute | solution.py:45
  5.1 13.8 %collective-permute-start.8 = (f32[256]{0:T(256)S(1)}, f32[256]{0:T(256)S(1)}, u32[]{:S(2)}, u32[]{:S(2)}) collective-permute-start(f32[256]{0:T(256)S(1)} %convert_reduce_fusion), channel_id=1, source_target_pairs={{0,1},{1,2},{2,3},{3,0},{4,5},{5,6},{6,7},{7,4},{8,9},{9,10},{10,1... | collective-permute-start | bytes 3080 | tf_op jit(solution)/shard_map/ppermute | solution.py:45
  7.5 11.4 %collective-permute-start.9 = (f32[256]{0:T(256)S(1)}, f32[256]{0:T(256)S(1)}, u32[]{:S(2)}, u32[]{:S(2)}) collective-permute-start(f32[256]{0:T(256)S(1)} %convert_reduce_fusion), channel_id=1, source_target_pairs={{0,2},{1,3},{2,0},{3,1},{4,6},{5,7},{6,4},{7,5},{8,10},{9,11},{10,... | collective-permute-start | bytes 3080 | tf_op jit(solution)/shard_map/ppermute | solution.py:45
  10.3 11.3 %collective-permute-start = (f32[2,8,8,256]{3,2,1,0:T(8,128)S(1)}, f32[2,8,8,256]{3,2,1,0:T(8,128)S(1)}, u32[]{:S(2)}, u32[]{:S(2)}) collective-permute-start(f32[2,8,8,256]{3,2,1,0:T(8,128)S(1)} %bitcast.39), channel_id=1, source_target_pairs={{0,16},{16,32},{32,48},{48,64},{64,80},{80,96},{96,112},{112,128},... | collective-permute-start | bytes 393224 | tf_op jit(solution)/shard_map/ppermute | solution.py:17
  13.4 9.3 %collective-permute-start.1 = (f32[2,8,8,256]{3,2,1,0:T(8,128)S(1)}, f32[2,8,8,256]{3,2,1,0:T(8,128)S(1)}, u32[]{:S(2)}, u32[]{:S(2)}) collective-permute-start(f32[2,8,8,256]{3,2,1,0:T(8,128)S(1)} %bitcast.38), channel_id=1, source_target_pairs={{16,0},{32,16},{48,32},{64,48},{80,64},{96,80},{112,96},{128,112},... | collective-permute-start | bytes 393224 | tf_op jit(solution)/shard_map/ppermute | solution.py:18
  18.9 9.3 %collective-permute-start.11 = (f32[256]{0:T(256)S(1)}, f32[256]{0:T(256)S(1)}, u32[]{:S(2)}, u32[]{:S(2)}) collective-permute-start(f32[256]{0:T(256)S(1)} %add_add_fusion.3), channel_id=1, source_target_pairs={{0,4},{4,8},{8,12},{12,0},{1,5},{5,9},{9,13},{13,1},{2,6},{6,10},{... | collective-permute-start | bytes 3080 | tf_op jit(solution)/shard_map/ppermute | solution.py:45
  19.0 9.2 %collective-permute-start.12 = (f32[256]{0:T(256)S(1)}, f32[256]{0:T(256)S(1)}, u32[]{:S(2)}, u32[]{:S(2)}) collective-permute-start(f32[256]{0:T(256)S(1)} %add_add_fusion.3), channel_id=1, source_target_pairs={{0,8},{4,12},{8,0},{12,4},{1,9},{5,13},{9,1},{13,5},{2,10},{6,14},... | collective-permute-start | bytes 3080 | tf_op jit(solution)/shard_map/ppermute | solution.py:45
  19.7 8.4 %collective-permute-start.13 = (f32[256]{0:T(256)S(1)}, f32[256]{0:T(256)S(1)}, u32[]{:S(2)}, u32[]{:S(2)}) collective-permute-start(f32[256]{0:T(256)S(1)} %add_add_fusion.3), channel_id=1, source_target_pairs={{0,12},{4,0},{8,4},{12,8},{1,13},{5,1},{9,5},{13,9},{2,14},{6,2},{... | collective-permute-start | bytes 3080 | tf_op jit(solution)/shard_map/ppermute | solution.py:45
  22.8 9.9 %collective-permute-start.3 = (f32[2,8,8,256]{3,2,1,0:T(8,128)S(1)}, f32[2,8,8,256]{3,2,1,0:T(8,128)S(1)}, u32[]{:S(2)}, u32[]{:S(2)}) collective-permute-start(f32[2,8,8,256]{3,2,1,0:T(8,128)S(1)} %slice.148), channel_id=1, source_target_pairs={{16,0},{32,16},{48,32},{64,48},{80,64},{96,80},{112,96},{128,112},... | collective-permute-start | bytes 393224 | tf_op jit(solution)/shard_map/ppermute | solution.py:18
  28.2 8.6 %collective-permute-start.2 = (f32[2,8,8,256]{3,2,1,0:T(8,128)S(1)}, f32[2,8,8,256]{3,2,1,0:T(8,128)S(1)}, u32[]{:S(2)}, u32[]{:S(2)}) collective-permute-start(f32[2,8,8,256]{3,2,1,0:T(8,128)S(1)} %get-tuple-element.27), channel_id=1, source_target_pairs={{0,16},{16,32},{32,48},{48,64},{64,80},{80,96},{96,112},{112,128},... | collective-permute-start | bytes 393224 | tf_op jit(solution)/shard_map/ppermute | solution.py:17
  28.2 10.4 %collective-permute-start.14 = (f32[256]{0:T(256)S(1)}, f32[256]{0:T(256)S(1)}, u32[]{:S(2)}, u32[]{:S(2)}) collective-permute-start(f32[256]{0:T(256)S(1)} %add_add_fusion.2), channel_id=1, source_target_pairs={{0,16},{16,32},{32,48},{48,0},{64,80},{80,96},{96,112},{112,64},{1... | collective-permute-start | bytes 3080 | tf_op jit(solution)/shard_map/ppermute | solution.py:45
  28.3 10.3 %collective-permute-start.15 = (f32[256]{0:T(256)S(1)}, f32[256]{0:T(256)S(1)}, u32[]{:S(2)}, u32[]{:S(2)}) collective-permute-start(f32[256]{0:T(256)S(1)} %add_add_fusion.2), channel_id=1, source_target_pairs={{0,32},{16,48},{32,0},{48,16},{64,96},{80,112},{96,64},{112,80},{1... | collective-permute-start | bytes 3080 | tf_op jit(solution)/shard_map/ppermute | solution.py:45
  29.3 9.3 %collective-permute-start.16 = (f32[256]{0:T(256)S(1)}, f32[256]{0:T(256)S(1)}, u32[]{:S(2)}, u32[]{:S(2)}) collective-permute-start(f32[256]{0:T(256)S(1)} %add_add_fusion.2), channel_id=1, source_target_pairs={{0,48},{16,0},{32,16},{48,32},{64,112},{80,64},{96,80},{112,96},{1... | collective-permute-start | bytes 3080 | tf_op jit(solution)/shard_map/ppermute | solution.py:45
  36.8 9.7 %collective-permute-start.4 = (f32[12,2,8,256]{3,2,1,0:T(8,128)S(1)}, f32[12,2,8,256]{3,2,1,0:T(8,128)S(1)}, u32[]{:S(2)}, u32[]{:S(2)}) collective-permute-start(f32[12,2,8,256]{3,2,1,0:T(8,128)S(1)} %get-tuple-element.32), channel_id=1, source_target_pairs={{0,4},{4,8},{8,12},{12,0},{1,5},{5,9},{9,13},{13,1},{2,6},{6,10},{... | collective-permute-start | bytes 589832 | tf_op jit(solution)/shard_map/ppermute | solution.py:17
  36.9 9.6 %collective-permute-start.5 = (f32[12,2,8,256]{3,2,1,0:T(8,128)S(1)}, f32[12,2,8,256]{3,2,1,0:T(8,128)S(1)}, u32[]{:S(2)}, u32[]{:S(2)}) collective-permute-start(f32[12,2,8,256]{3,2,1,0:T(8,128)S(1)} %get-tuple-element.33), channel_id=1, source_target_pairs={{4,0},{8,4},{12,8},{0,12},{5,1},{9,5},{13,9},{1,13},{6,2},{10,6},{... | collective-permute-start | bytes 589832 | tf_op jit(solution)/shard_map/ppermute | solution.py:18
  38.6 10.3 %collective-permute-start.17 = (f32[256]{0:T(256)S(1)}, f32[256]{0:T(256)S(1)}, u32[]{:S(2)}, u32[]{:S(2)}) collective-permute-start(f32[256]{0:T(256)S(1)} %add_add_fusion.1), channel_id=1, source_target_pairs={{0,64},{16,80},{32,96},{48,112},{64,128},{80,144},{96,160},{112,17... | collective-permute-start | bytes 3080 | tf_op jit(solution)/shard_map/ppermute | solution.py:45
  41.0 7.9 %collective-permute-start.18 = (f32[256]{0:T(256)S(1)}, f32[256]{0:T(256)S(1)}, u32[]{:S(2)}, u32[]{:S(2)}) collective-permute-start(f32[256]{0:T(256)S(1)} %add_add_fusion.1), channel_id=1, source_target_pairs={{0,128},{16,144},{32,160},{48,176},{64,192},{80,208},{96,224},{112... | collective-permute-start | bytes 3080 | tf_op jit(solution)/shard_map/ppermute | solution.py:45
  43.4 5.5 %collective-permute-start.19 = (f32[256]{0:T(256)S(1)}, f32[256]{0:T(256)S(1)}, u32[]{:S(2)}, u32[]{:S(2)}) collective-permute-start(f32[256]{0:T(256)S(1)} %add_add_fusion.1), channel_id=1, source_target_pairs={{0,192},{16,208},{32,224},{48,240},{64,0},{80,16},{96,32},{112,48}... | collective-permute-start | bytes 3080 | tf_op jit(solution)/shard_map/ppermute | solution.py:45
  46.7 8.1 %collective-permute-start.6 = (f32[12,12,2,256]{3,2,1,0:T(2,128)S(1)}, f32[12,12,2,256]{3,2,1,0:T(2,128)S(1)}, u32[]{:S(2)}, u32[]{:S(2)}) collective-permute-start(f32[12,12,2,256]{3,2,1,0:T(2,128)S(1)} %get-tuple-element.31), channel_id=1, source_target_pairs={{0,1},{1,2},{2,3},{3,0},{4,5},{5,6},{6,7},{7,4},{8,9},{9,10},{10,1... | collective-permute-start | bytes 884744 | tf_op jit(solution)/shard_map/ppermute | solution.py:17
  48.9 9.0 %collective-permute-start.7 = (f32[12,12,2,256]{3,2,1,0:T(2,128)S(1)}, f32[12,12,2,256]{3,2,1,0:T(2,128)S(1)}, u32[]{:S(2)}, u32[]{:S(2)}) collective-permute-start(f32[12,12,2,256]{3,2,1,0:T(2,128)S(1)} %get-tuple-element.30), channel_id=1, source_target_pairs={{1,0},{2,1},{3,2},{0,3},{5,4},{6,5},{7,6},{4,7},{9,8},{10,9},{11,1... | collective-permute-start | bytes 884744 | tf_op jit(solution)/shard_map/ppermute | solution.py:18
  59.0 2.9 %copy-start.1 = (bf16[256,256]{1,0:T(8,128)(2,1)S(1)}, bf16[256,256]{1,0:T(8,128)(2,1)}, u32[]{:S(2)}) copy-start(bf16[256,256]{1,0:T(8,128)(2,1)} %base_ref.1) | copy-start | bytes 393220
  59.0 2.9 %copy-start.2 = (f32[98,256]{1,0:T(8,128)S(1)}, f32[98,256]{1,0:T(8,128)}, u32[]{:S(2)}) copy-start(f32[98,256]{1,0:T(8,128)} %rs_ref.1) | copy-start | bytes 301060
  59.0 2.9 %copy-start.3 = (f32[98,256]{1,0:T(8,128)S(1)}, f32[98,256]{1,0:T(8,128)}, u32[]{:S(2)}) copy-start(f32[98,256]{1,0:T(8,128)} %cs_ref.1) | copy-start | bytes 301060
  59.0 2.9 %copy-start.4 = (s32[294]{0:T(512)S(1)}, s32[294]{0:T(512)}, u32[]{:S(2)}) copy-start(s32[294]{0:T(512)} %constant.59.clone.tab_ref) | copy-start | bytes 3532
  59.3 2.6 %copy-start.5 = (f32[5,12,12,8,256]{4,3,2,1,0:T(8,128)}, f32[5,12,12,8,256]{4,3,2,1,0:T(8,128)S(1)}, u32[]{:S(2)}) copy-start(f32[5,12,12,8,256]{4,3,2,1,0:T(8,128)S(1)} %fusion.8.ysh_ref) | copy-start | bytes 17694724
  94.7 8.0 %collective-permute-start.20 = (bf16[2,8,8,256]{3,2,1,0:T(8,128)(2,1)S(1)}, bf16[2,8,8,256]{3,2,1,0:T(8,128)(2,1)S(1)}, u32[]{:S(2)}, u32[]{:S(2)}) collective-permute-start(bf16[2,8,8,256]{3,2,1,0:T(8,128)(2,1)S(1)} %bitcast.41), channel_id=1, source_target_pairs={{0,16},{16,32},{32,48},{48,64},{64,80},{80,96},{96,112},{112,128},... | collective-permute-start | bytes 196616 | tf_op jit(solution)/shard_map/ppermute | solution.py:17
  94.8 7.9 %collective-permute-start.21 = (bf16[2,8,8,256]{3,2,1,0:T(8,128)(2,1)S(1)}, bf16[2,8,8,256]{3,2,1,0:T(8,128)(2,1)S(1)}, u32[]{:S(2)}, u32[]{:S(2)}) collective-permute-start(bf16[2,8,8,256]{3,2,1,0:T(8,128)(2,1)S(1)} %bitcast.40), channel_id=1, source_target_pairs={{16,0},{32,16},{48,32},{64,48},{80,64},{96,80},{112,96},{128,112},... | collective-permute-start | bytes 196616 | tf_op jit(solution)/shard_map/ppermute | solution.py:18
where the time goes:
time: 108 us
  starting transfers between devices  41.8 us (39%)
  Pallas kernels  31.9 us (30%)
  waiting for transfers between devices  16.6 us (15%)
  local copies, waits for them, and re-layouts  7.27 us (7%)
  matrix products  6.82 us (6%)
  other arithmetic  2.52 us (2%)
    pallas_call x1, Pallas kernels, far_field(): pl.pallas_call(far_kernel, out_shape=jax.ShapeDtypeStruct((rows, componen...  31.9 us
    ppermute x12, starting transfers between devices, axis_sum(): total = total + lax.ppermute(x, axis, pairs)  18.3 us
    ppermute x5, starting transfers between devices, padded_2(): after = lax.ppermute(leading, axis, down)  18.1 us
    ppermute x5, waiting for transfers between devices, padded_2(): before = lax.ppermute(last, axis, up)  12.5 us
    unnamed x24, local copies, waits for them, and re-layouts  5.98 us
    ppermute x5, starting transfers between devices, padded_2(): before = lax.ppermute(last, axis, up)  5.39 us
    dot_general x1, matrix products, per_device(): jnp.dot(onehot, flat_locals, preferred_element_type=jnp.float32)  4.26 us
    ppermute x5, waiting for transfers between devices, padded_2(): after = lax.ppermute(leading, axis, down)  4.08 us
  transfers between devices with their start and end apart: 22, of which 6 were waited for; matrix products, arithmetic and copies ran while one was open for 3% of the time, Pallas kernels for 0%

commit v1 on v0

--- a/solution.py
+++ b/solution.py
@@ -51,21 +51,28 @@
 def far_kernel(tab_ref, ysh_ref, mask_ref, rs_ref, cs_ref, base_ref, lat_ref, out_ref, acc_ref):
     rows = acc_ref.shape[0]
     lanes = mask_ref.shape[1]
+    levels = 2
+    chunk = levels * 8 * ysh_ref.shape[3]
     acc_ref[...] = jnp.zeros(acc_ref.shape, jnp.float32)
-    lane = lax.broadcasted_iota(jnp.int32, (rows, lanes), 1)
+    lane = lax.broadcasted_iota(jnp.int32, (chunk, lanes), 1)
 
     def body(o, carry):
         a = tab_ref[3 * o]
         b = tab_ref[3 * o + 1]
         c = tab_ref[3 * o + 2]
-        win = ysh_ref[c, pl.ds(a, 8), pl.ds(b, 8), :, :].reshape(rows, -1)
-        gate = jnp.sum(jnp.where(lane == o, mask_ref[...], 0.0), axis=1, keepdims=True)
-        scaled = (win * gate * rs_ref[pl.ds(o, 1), :]).astype(jnp.bfloat16)
-        product = jnp.dot(scaled, base_ref[...], preferred_element_type=jnp.float32)
-        acc_ref[...] += product * cs_ref[pl.ds(o, 1), :]
+        row_scale = rs_ref[pl.ds(o, 1), :]
+        col_scale = cs_ref[pl.ds(o, 1), :]
+        for q in range(rows // chunk):
+            win = ysh_ref[c, pl.ds(a + levels * q, levels), pl.ds(b, 8), :, :].reshape(chunk, -1)
+            gate = jnp.sum(
+                jnp.where(lane == o, mask_ref[q * chunk : (q + 1) * chunk, :], 0.0), axis=1, keepdims=True
+            )
+            scaled = (win * gate * row_scale).astype(jnp.bfloat16)
+            product = jnp.dot(scaled, base_ref[...], preferred_element_type=jnp.float32)
+            acc_ref[q * chunk : (q + 1) * chunk, :] += product * col_scale
         return carry
 
-    lax.fori_loop(0, tab_ref.shape[0] // 3, body, 0)
+    lax.fori_loop(0, tab_ref.shape[0] // 3, body, 0, unroll=2)
     out_ref[...] = (acc_ref[...] + lat_ref[...]).astype(out_ref.dtype)
 
 
@@ -101,11 +108,13 @@
     selector = (labels[:, None] == pair_box[None, :]).astype(jnp.bfloat16)
     partial_near = jnp.dot(selector, weighted, preferred_element_type=jnp.float32)
     partial_near = partial_near.reshape(depth + 4, width_x, width_y, components)
-    bordered = padded_2(partial_near, (("rows", 0),), 2)
-    stored = partial_near[2 : 2 + depth]
-    stored = stored.at[:2].add(bordered[:2])
-    stored = stored.at[depth - 2 :].add(bordered[depth + 6 :])
-    padded = padded_2(stored, (("rows", 0), ("bx", 1), ("by", 2)), 2)
+    count = lax.axis_size("rows")
+    up = [(i, (i + 1) % count) for i in range(count)]
+    down = [(j, i) for i, j in up]
+    from_below = lax.ppermute(partial_near[depth:], "rows", up)
+    from_above = lax.ppermute(partial_near[:4], "rows", down)
+    zpad = partial_near.at[:4].add(from_below).at[depth:].add(from_above)
+    padded = padded_2(zpad, (("bx", 1), ("by", 2)), 2)
     ysh = jnp.stack([padded[:, :, c : c + width_y] for c in range(5)])
     masks = inter_mask.reshape(depth * width_x * width_y, offsets).astype(jnp.float32)
     far = far_field(ysh, masks, row_scale, col_scale, base, lattice_term)

time: 108 us -> 96.8 us (0.90)
  Pallas kernels: 31.9 us -> 21.9 us
  waiting for transfers between devices: 16.6 us -> 14.2 us
  starting transfers between devices: 41.8 us -> 42.9 us
    ppermute x5 -> x3, starting transfers between devices: 18.1 us -> 4.81 us  [padded_2(): after = lax.ppermute(leading, axis, down)]
    ppermute x0 -> x2, starting transfers between devices: none -> 11.1 us  [the longest x1 8.06 us: per_device(): from_above = lax.ppermute(partial_near[:4], 'rows', down)]
    pallas_call x1, Pallas kernels: 31.9 us -> 21.9 us  [far_field(): pl.pallas_call(far_kernel, out_shape=jax.ShapeDtypeStruct((rows, componen...]
    ppermute x5 -> x3, waiting for transfers between devices: 12.5 us -> 7.36 us  [padded_2(): before = lax.ppermute(last, axis, up)]
    ppermute x5 -> x3, starting transfers between devices: 5.39 us -> 9.74 us  [padded_2(): before = lax.ppermute(last, axis, up)]
    ppermute x0 -> x2, waiting for transfers between devices: none -> 2.72 us  [the longest x1 2.72 us: per_device(): from_above = lax.ppermute(partial_near[:4], 'rows', down)]
    ppermute x5 -> x3, waiting for transfers between devices: 4.08 us -> 4.08 us  [padded_2(): after = lax.ppermute(leading, axis, down)]
  transfers between devices with their start and end apart: 22 -> 20, of which waited for: 6 -> 5; matrix products, arithmetic and copies ran while one was open for 3% -> 3% of each run, Pallas kernels for 0% -> 0%
where the time goes in v1:
time: 96.8 us; the launch traced here: 96.5 us
  starting transfers between devices  42.9 us (44%)
  Pallas kernels  21.9 us (23%)
  waiting for transfers between devices  14.2 us (15%)
  local copies, waits for them, and re-layouts  7.29 us (8%)
  matrix products  6.82 us (7%)
  other arithmetic  2.46 us (3%)
  between operations  0.97 us (1%)
    pallas_call x1, Pallas kernels, far_field(): pl.pallas_call(far_kernel, out_shape=jax.ShapeDtypeStruct((rows, componen...  21.9 us
    ppermute x12, starting transfers between devices, axis_sum(): total = total + lax.ppermute(x, axis, pairs)  17.3 us
    ppermute x3, starting transfers between devices, padded_2(): before = lax.ppermute(last, axis, up)  9.74 us
    ppermute x1, starting transfers between devices, per_device(): from_above = lax.ppermute(partial_near[:4], 'rows', down)  8.06 us
    ppermute x3, waiting for transfers between devices, padded_2(): before = lax.ppermute(last, axis, up)  7.36 us
    unnamed x24, local copies, waits for them, and re-layouts  6 us
    ppermute x3, starting transfers between devices, padded_2(): after = lax.ppermute(leading, axis, down)  4.81 us
    dot_general x1, matrix products, per_device(): jnp.dot(onehot, flat_locals, preferred_element_type=jnp.float32)  4.26 us
  transfers between devices with their start and end apart: 20, of which 5 were waited for; matrix products, arithmetic and copies ran while one was open for 3% of the time, Pallas kernels for 0%

profile of v1, /device:TPU:6, one launch (start us, length us, event | category | flops | bytes accessed | tf_op | source)
XLA Modules:
  0.0 96.5 jit_solution(15291168523896738845)
XLA Ops:
  0.6 0.0 copy-start
  0.7 3.0 %copy.12 = bf16[4096,256]{0,1:T(8,128)(2,1)S(1)} copy(bf16[4096,256]{1,0:T(8,128)(2,1)} %param.14) | data formatting | bytes 4194304 | tf_op args[0]
  3.6 0.0 copy-done.7
  3.7 0.5 convert_reduce_fusion
  4.2 2.3 %collective-permute-start.6 = (f32[256]{0:T(256)S(1)}, f32[256]{0:T(256)S(1)}, u32[]{:S(2)}, u32[]{:S(2)}) collective-permute-start(f32[256]{0:T(256)S(1)} %convert_reduce_fusion), channel_id=1, source_target_pairs={{0,1},{1,2},{2,3},{3,0},{4,5},{5,6},{6,7},{7,4},{8,9},{9,10},{10,1... | collective-permute-start | bytes 3080 | tf_op jit(solution)/shard_map/ppermute | solution.py:45
  6.4 0.7 collective-permute-start.7
  7.2 0.2 collective-permute-start.8
  7.4 2.4 %fusion = f32[768,256]{1,0:T(8,128)S(1)} fusion(s32[4096]{0:T(1024)S(1)} %copy-done.9, bf16[4096,256]{0,1:T(8,128)(2,1)S(1)} %copy.12, f32[4096]{0:T(1024)S(1)} %convert_multiply_fusion.1), kind=kOutput, calls=%fused_computation.2 | convolution fusion | flops 1616904192 | bytes 2916352 | tf_op jit(solution)/shard_map/dot_general | solution.py:109
  9.8 3.0 %collective-permute-start = (f32[4,8,8,256]{3,2,1,0:T(8,128)S(1)}, f32[4,8,8,256]{3,2,1,0:T(8,128)S(1)}, u32[]{:S(2)}, u32[]{:S(2)}) collective-permute-start(f32[4,8,8,256]{3,2,1,0:T(8,128)S(1)} %bitcast.38), channel_id=1, source_target_pairs={{0,16},{16,32},{32,48},{48,64},{64,80},{80,96},{96,112},{112,128},... | collective-permute-start | bytes 786440 | tf_op jit(solution)/shard_map/ppermute | solution.py:114
  12.9 0.0 collective-permute-done.6
  12.9 0.0 collective-permute-done.7
  12.9 0.0 collective-permute-done.8
  12.9 0.8 collective-permute-start.10
  13.7 0.0 collective-permute-start.11
  13.7 0.5 collective-permute-start.9
  14.2 8.1 %collective-permute-start.1 = (f32[4,8,8,256]{3,2,1,0:T(8,128)S(1)}, f32[4,8,8,256]{3,2,1,0:T(8,128)S(1)}, u32[]{:S(2)}, u32[]{:S(2)}) collective-permute-start(f32[4,8,8,256]{3,2,1,0:T(8,128)S(1)} %bitcast.35), channel_id=1, source_target_pairs={{16,0},{32,16},{48,32},{64,48},{80,64},{96,80},{112,96},{128,112},... | collective-permute-start | bytes 786440 | tf_op jit(solution)/shard_map/ppermute | solution.py:115
  22.3 0.0 collective-permute-done.10
  22.3 0.0 collective-permute-done.11
  22.3 0.0 collective-permute-done.9
  22.3 0.1 collective-permute-start.12
  22.4 0.1 collective-permute-start.13
  22.5 4.3 %collective-permute-start.14 = (f32[256]{0:T(256)S(1)}, f32[256]{0:T(256)S(1)}, u32[]{:S(2)}, u32[]{:S(2)}) collective-permute-start(f32[256]{0:T(256)S(1)} %add_add_fusion.2), channel_id=1, source_target_pairs={{0,48},{16,0},{32,16},{48,32},{64,112},{80,64},{96,80},{112,96},{1... | collective-permute-start | bytes 3080 | tf_op jit(solution)/shard_map/ppermute | solution.py:45
  26.8 0.0 collective-permute-done
  26.9 2.7 %collective-permute-done.1 = f32[4,8,8,256]{3,2,1,0:T(8,128)S(1)} collective-permute-done((f32[4,8,8,256]{3,2,1,0:T(8,128)S(1)}, f32[4,8,8,256]{3,2,1,0:T(8,128)S(1)}, u32[]{:S(2)}, u32[]{:S(2)}) %collective-permute-start.1) | collective-permute-done | bytes 262176 | tf_op jit(solution)/shard_map/ppermute | solution.py:115
  29.6 0.1 fusion.12
  29.7 0.4 collective-permute-start.2
  30.0 1.6 %collective-permute-start.3 = (f32[12,2,8,256]{3,2,1,0:T(8,128)S(1)}, f32[12,2,8,256]{3,2,1,0:T(8,128)S(1)}, u32[]{:S(2)}, u32[]{:S(2)}) collective-permute-start(f32[12,2,8,256]{3,2,1,0:T(8,128)S(1)} %get-tuple-element.31), channel_id=1, source_target_pairs={{4,0},{8,4},{12,8},{0,12},{5,1},{9,5},{13,9},{1,13},{6,2},{10,6},{... | collective-permute-start | bytes 589832 | tf_op jit(solution)/shard_map/ppermute | solution.py:18
  31.7 0.0 collective-permute-done.12
  31.7 0.0 collective-permute-done.13
  31.7 0.0 collective-permute-done.14
  31.7 0.1 collective-permute-start.15
  31.8 4.3 %collective-permute-start.16 = (f32[256]{0:T(256)S(1)}, f32[256]{0:T(256)S(1)}, u32[]{:S(2)}, u32[]{:S(2)}) collective-permute-start(f32[256]{0:T(256)S(1)} %add_add_fusion.1), channel_id=1, source_target_pairs={{0,128},{16,144},{32,160},{48,176},{64,192},{80,208},{96,224},{112... | collective-permute-start | bytes 3080 | tf_op jit(solution)/shard_map/ppermute | solution.py:45
  36.1 3.9 %collective-permute-start.17 = (f32[256]{0:T(256)S(1)}, f32[256]{0:T(256)S(1)}, u32[]{:S(2)}, u32[]{:S(2)}) collective-permute-start(f32[256]{0:T(256)S(1)} %add_add_fusion.1), channel_id=1, source_target_pairs={{0,192},{16,208},{32,224},{48,240},{64,0},{80,16},{96,32},{112,48}... | collective-permute-start | bytes 3080 | tf_op jit(solution)/shard_map/ppermute | solution.py:45
  40.0 0.0 collective-permute-done.2
  40.0 0.0 collective-permute-done.3
  40.0 0.1 pad_maximum_fusion.1
  40.1 0.2 fusion.13
  40.3 6.8 %collective-permute-start.4 = (f32[12,12,2,256]{3,2,1,0:T(2,128)S(1)}, f32[12,12,2,256]{3,2,1,0:T(2,128)S(1)}, u32[]{:S(2)}, u32[]{:S(2)}) collective-permute-start(f32[12,12,2,256]{3,2,1,0:T(2,128)S(1)} %get-tuple-element.29), channel_id=1, source_target_pairs={{0,1},{1,2},{2,3},{3,0},{4,5},{5,6},{6,7},{7,4},{8,9},{9,10},{10,1... | collective-permute-start | bytes 884744 | tf_op jit(solution)/shard_map/ppermute | solution.py:17
  47.1 0.0 collective-permute-start.5
  47.1 0.0 collective-permute-done.15
  47.1 0.0 collective-permute-done.16
  47.1 0.0 collective-permute-done.17
  47.1 0.2 fusion.17.lat_ref
  47.3 5.1 %collective-permute-done.4 = f32[12,12,2,256]{3,2,1,0:T(2,128)S(1)} collective-permute-done((f32[12,12,2,256]{3,2,1,0:T(2,128)S(1)}, f32[12,12,2,256]{3,2,1,0:T(2,128)S(1)}, u32[]{:S(2)}, u32[]{:S(2)}) %collective-permute-start.4) | collective-permute-done | bytes 294944 | tf_op jit(solution)/shard_map/ppermute | solution.py:17
  52.4 3.4 %collective-permute-done.5 = f32[12,12,2,256]{3,2,1,0:T(2,128)S(1)} collective-permute-done((f32[12,12,2,256]{3,2,1,0:T(2,128)S(1)}, f32[12,12,2,256]{3,2,1,0:T(2,128)S(1)}, u32[]{:S(2)}, u32[]{:S(2)}) %collective-permute-start.5) | collective-permute-done | bytes 294944 | tf_op jit(solution)/shard_map/ppermute | solution.py:18
  55.8 0.7 pad_maximum_fusion
  56.5 0.1 fusion.11
  56.6 0.2 fusion.10
  56.8 0.1 bitcast_dynamic-update-slice_fusion
  56.9 0.0 copy-start.1
  56.9 0.0 copy-start.2
  56.9 0.0 copy-start.3
  56.9 0.0 copy-start.4
  56.9 0.2 fusion.9
  57.1 0.2 fusion.8.ysh_ref
  57.3 2.5 %copy-done.5 = f32[5,12,12,8,256]{4,3,2,1,0:T(8,128)} copy-done((f32[5,12,12,8,256]{4,3,2,1,0:T(8,128)}, f32[5,12,12,8,256]{4,3,2,1,0:T(8,128)S(1)}, u32[]{:S(2)}) %copy-start.5) | copy-done | bytes 5898264
  59.8 21.9 %shard_map.113 = bf16[512,256]{1,0:T(8,128)(2,1)} custom-call(s32[294]{0:T(512)S(1)} %copy-done.4, f32[5,12,12,8,256]{4,3,2,1,0:T(8,128)} %copy-done.5, f32[512,98]{1,0:T(8,128)S(1)} %bitcast.31, f32[98,256]{1,0:T(8,128)S(1)} %copy-done.2, f32[98,256]{1,0:T(8,128)S(1)} %copy-done.3, bf16[256,256]{1,0:T(8,128)(2,1)S(1)} %copy-done.1, f32[1,256]{1,0:T(1,128)S(1)} %fusion.17.lat_ref), custom_call_target="tpu_custom_call" | custom-call | tf_op jit(solution)/shard_map/pallas_call | solution.py:85
  81.7 0.9 fusion.16
  82.6 2.5 %collective-permute-start.18 = (bf16[2,8,8,256]{3,2,1,0:T(8,128)(2,1)S(1)}, bf16[2,8,8,256]{3,2,1,0:T(8,128)(2,1)S(1)}, u32[]{:S(2)}, u32[]{:S(2)}) collective-permute-start(bf16[2,8,8,256]{3,2,1,0:T(8,128)(2,1)S(1)} %bitcast.40), channel_id=1, source_target_pairs={{0,16},{16,32},{32,48},{48,64},{64,80},{80,96},{96,112},{112,128},... | collective-permute-start | bytes 196616 | tf_op jit(solution)/shard_map/ppermute | solution.py:17
  85.2 3.2 %collective-permute-start.19 = (bf16[2,8,8,256]{3,2,1,0:T(8,128)(2,1)S(1)}, bf16[2,8,8,256]{3,2,1,0:T(8,128)(2,1)S(1)}, u32[]{:S(2)}, u32[]{:S(2)}) collective-permute-start(bf16[2,8,8,256]{3,2,1,0:T(8,128)(2,1)S(1)} %bitcast.39), channel_id=1, source_target_pairs={{16,0},{32,16},{48,32},{64,48},{80,64},{96,80},{112,96},{128,112},... | collective-permute-start | bytes 196616 | tf_op jit(solution)/shard_map/ppermute | solution.py:18
  88.3 2.3 %collective-permute-done.18 = bf16[2,8,8,256]{3,2,1,0:T(8,128)(2,1)S(1)} collective-permute-done((bf16[2,8,8,256]{3,2,1,0:T(8,128)(2,1)S(1)}, bf16[2,8,8,256]{3,2,1,0:T(8,128)(2,1)S(1)}, u32[]{:S(2)}, u32[]{:S(2)}) %collective-permute-start.18) | collective-permute-done | bytes 65568 | tf_op jit(solution)/shard_map/ppermute | solution.py:17
  90.6 0.7 collective-permute-done.19
  91.3 1.0 %pad_maximum_fusion.2 = bf16[12,8,8,256]{3,2,1,0:T(8,128)(2,1)S(1)} fusion(bf16[2,8,8,256]{3,2,1,0:T(8,128)(2,1)S(1)} %collective-permute-done.19, bf16[8,8,8,256]{3,2,1,0:T(8,128)(2,1)} %bitcast.33, bf16[2,8,8,256]{3,2,1,0:T(8,128)(2,1)S(1)} %collective-permute-done.18), kind=kLoop, calls=%fused_computation.23 | loop fusion | flops 393216 | bytes 786432 | tf_op jit(solution)/shard_map/concatenate | solution.py:19
  92.3 4.3 %fusion.7 = f32[4096]{0:T(1024)} fusion(bf16[768,256]{1,0:T(8,128)(2,1)S(1)} %bitcast.37, s32[4096]{0:T(1024)S(1)} %copy-done.9, bf16[4096,256]{0,1:T(8,128)(2,1)S(1)} %copy.12), kind=kOutput, calls=%fused_computation.12 | convolution fusion | flops 1616900096 | bytes 2523136 | tf_op jit(solution)/shard_map/dot_general | solution.py:125
  (22 shorter events, 0.2 us)
Async XLA Ops:
  0.6 46.5 %copy-start = (f32[256,256]{1,0:T(8,128)S(1)}, f32[256,256]{1,0:T(8,128)}, u32[]{:S(2)}) copy-start(f32[256,256]{1,0:T(8,128)} %param.22) | copy-start | bytes 786436
  0.6 3.0 %copy-start.7 = (f32[4096]{0:T(1024)S(1)}, f32[4096]{0:T(1024)}, u32[]{:S(2)}) copy-start(f32[4096]{0:T(1024)} %param.15) | copy-start | bytes 49156
  0.7 3.0 %copy-start.8 = (s32[4096]{0:T(1024)S(1)}, s32[4096]{0:T(1024)}, u32[]{:S(2)}) copy-start(s32[4096]{0:T(1024)} %param.16) | copy-start | bytes 49156
  0.7 6.7 %copy-start.9 = (s32[4096]{0:T(1024)S(1)}, s32[4096]{0:T(1024)}, u32[]{:S(2)}) copy-start(s32[4096]{0:T(1024)} %param.17) | copy-start | bytes 49156
  4.2 18.1 %copy-start.6 = (s32[8,8,8,98]{3,2,1,0:T(8,128)S(1)}, s32[8,8,8,98]{3,2,1,0:T(8,128)}, u32[]{:S(2)}) copy-start(s32[8,8,8,98]{3,2,1,0:T(8,128)} %param.18) | copy-start | bytes 602116
  4.2 8.7 %collective-permute-start.6 = (f32[256]{0:T(256)S(1)}, f32[256]{0:T(256)S(1)}, u32[]{:S(2)}, u32[]{:S(2)}) collective-permute-start(f32[256]{0:T(256)S(1)} %convert_reduce_fusion), channel_id=1, source_target_pairs={{0,1},{1,2},{2,3},{3,0},{4,5},{5,6},{6,7},{7,4},{8,9},{9,10},{10,1... | collective-permute-start | bytes 3080 | tf_op jit(solution)/shard_map/ppermute | solution.py:45
  6.4 6.4 %collective-permute-start.7 = (f32[256]{0:T(256)S(1)}, f32[256]{0:T(256)S(1)}, u32[]{:S(2)}, u32[]{:S(2)}) collective-permute-start(f32[256]{0:T(256)S(1)} %convert_reduce_fusion), channel_id=1, source_target_pairs={{0,2},{1,3},{2,0},{3,1},{4,6},{5,7},{6,4},{7,5},{8,10},{9,11},{10,... | collective-permute-start | bytes 3080 | tf_op jit(solution)/shard_map/ppermute | solution.py:45
  7.2 5.7 %collective-permute-start.8 = (f32[256]{0:T(256)S(1)}, f32[256]{0:T(256)S(1)}, u32[]{:S(2)}, u32[]{:S(2)}) collective-permute-start(f32[256]{0:T(256)S(1)} %convert_reduce_fusion), channel_id=1, source_target_pairs={{0,3},{1,0},{2,1},{3,2},{4,7},{5,4},{6,5},{7,6},{8,11},{9,8},{10,9... | collective-permute-start | bytes 3080 | tf_op jit(solution)/shard_map/ppermute | solution.py:45
  9.8 17.0 %collective-permute-start = (f32[4,8,8,256]{3,2,1,0:T(8,128)S(1)}, f32[4,8,8,256]{3,2,1,0:T(8,128)S(1)}, u32[]{:S(2)}, u32[]{:S(2)}) collective-permute-start(f32[4,8,8,256]{3,2,1,0:T(8,128)S(1)} %bitcast.38), channel_id=1, source_target_pairs={{0,16},{16,32},{32,48},{48,64},{64,80},{80,96},{96,112},{112,128},... | collective-permute-start | bytes 786440 | tf_op jit(solution)/shard_map/ppermute | solution.py:114
  12.9 9.4 %collective-permute-start.10 = (f32[256]{0:T(256)S(1)}, f32[256]{0:T(256)S(1)}, u32[]{:S(2)}, u32[]{:S(2)}) collective-permute-start(f32[256]{0:T(256)S(1)} %add_add_fusion.3), channel_id=1, source_target_pairs={{0,8},{4,12},{8,0},{12,4},{1,9},{5,13},{9,1},{13,5},{2,10},{6,14},... | collective-permute-start | bytes 3080 | tf_op jit(solution)/shard_map/ppermute | solution.py:45
  13.7 8.6 %collective-permute-start.11 = (f32[256]{0:T(256)S(1)}, f32[256]{0:T(256)S(1)}, u32[]{:S(2)}, u32[]{:S(2)}) collective-permute-start(f32[256]{0:T(256)S(1)} %add_add_fusion.3), channel_id=1, source_target_pairs={{0,12},{4,0},{8,4},{12,8},{1,13},{5,1},{9,5},{13,9},{2,14},{6,2},{... | collective-permute-start | bytes 3080 | tf_op jit(solution)/shard_map/ppermute | solution.py:45
  13.7 8.6 %collective-permute-start.9 = (f32[256]{0:T(256)S(1)}, f32[256]{0:T(256)S(1)}, u32[]{:S(2)}, u32[]{:S(2)}) collective-permute-start(f32[256]{0:T(256)S(1)} %add_add_fusion.3), channel_id=1, source_target_pairs={{0,4},{4,8},{8,12},{12,0},{1,5},{5,9},{9,13},{13,1},{2,6},{6,10},{... | collective-permute-start | bytes 3080 | tf_op jit(solution)/shard_map/ppermute | solution.py:45
  14.2 15.4 %collective-permute-start.1 = (f32[4,8,8,256]{3,2,1,0:T(8,128)S(1)}, f32[4,8,8,256]{3,2,1,0:T(8,128)S(1)}, u32[]{:S(2)}, u32[]{:S(2)}) collective-permute-start(f32[4,8,8,256]{3,2,1,0:T(8,128)S(1)} %bitcast.35), channel_id=1, source_target_pairs={{16,0},{32,16},{48,32},{64,48},{80,64},{96,80},{112,96},{128,112},... | collective-permute-start | bytes 786440 | tf_op jit(solution)/shard_map/ppermute | solution.py:115
  22.3 9.4 %collective-permute-start.12 = (f32[256]{0:T(256)S(1)}, f32[256]{0:T(256)S(1)}, u32[]{:S(2)}, u32[]{:S(2)}) collective-permute-start(f32[256]{0:T(256)S(1)} %add_add_fusion.2), channel_id=1, source_target_pairs={{0,16},{16,32},{32,48},{48,0},{64,80},{80,96},{96,112},{112,64},{1... | collective-permute-start | bytes 3080 | tf_op jit(solution)/shard_map/ppermute | solution.py:45
  22.4 9.3 %collective-permute-start.13 = (f32[256]{0:T(256)S(1)}, f32[256]{0:T(256)S(1)}, u32[]{:S(2)}, u32[]{:S(2)}) collective-permute-start(f32[256]{0:T(256)S(1)} %add_add_fusion.2), channel_id=1, source_target_pairs={{0,32},{16,48},{32,0},{48,16},{64,96},{80,112},{96,64},{112,80},{1... | collective-permute-start | bytes 3080 | tf_op jit(solution)/shard_map/ppermute | solution.py:45
  22.5 9.2 %collective-permute-start.14 = (f32[256]{0:T(256)S(1)}, f32[256]{0:T(256)S(1)}, u32[]{:S(2)}, u32[]{:S(2)}) collective-permute-start(f32[256]{0:T(256)S(1)} %add_add_fusion.2), channel_id=1, source_target_pairs={{0,48},{16,0},{32,16},{48,32},{64,112},{80,64},{96,80},{112,96},{1... | collective-permute-start | bytes 3080 | tf_op jit(solution)/shard_map/ppermute | solution.py:45
  29.7 10.3 %collective-permute-start.2 = (f32[12,2,8,256]{3,2,1,0:T(8,128)S(1)}, f32[12,2,8,256]{3,2,1,0:T(8,128)S(1)}, u32[]{:S(2)}, u32[]{:S(2)}) collective-permute-start(f32[12,2,8,256]{3,2,1,0:T(8,128)S(1)} %get-tuple-element.30), channel_id=1, source_target_pairs={{0,4},{4,8},{8,12},{12,0},{1,5},{5,9},{9,13},{13,1},{2,6},{6,10},{... | collective-permute-start | bytes 589832 | tf_op jit(solution)/shard_map/ppermute | solution.py:17
  30.0 10.0 %collective-permute-start.3 = (f32[12,2,8,256]{3,2,1,0:T(8,128)S(1)}, f32[12,2,8,256]{3,2,1,0:T(8,128)S(1)}, u32[]{:S(2)}, u32[]{:S(2)}) collective-permute-start(f32[12,2,8,256]{3,2,1,0:T(8,128)S(1)} %get-tuple-element.31), channel_id=1, source_target_pairs={{4,0},{8,4},{12,8},{0,12},{5,1},{9,5},{13,9},{1,13},{6,2},{10,6},{... | collective-permute-start | bytes 589832 | tf_op jit(solution)/shard_map/ppermute | solution.py:18
  31.7 15.4 %collective-permute-start.15 = (f32[256]{0:T(256)S(1)}, f32[256]{0:T(256)S(1)}, u32[]{:S(2)}, u32[]{:S(2)}) collective-permute-start(f32[256]{0:T(256)S(1)} %add_add_fusion.1), channel_id=1, source_target_pairs={{0,64},{16,80},{32,96},{48,112},{64,128},{80,144},{96,160},{112,17... | collective-permute-start | bytes 3080 | tf_op jit(solution)/shard_map/ppermute | solution.py:45
  31.8 15.3 %collective-permute-start.16 = (f32[256]{0:T(256)S(1)}, f32[256]{0:T(256)S(1)}, u32[]{:S(2)}, u32[]{:S(2)}) collective-permute-start(f32[256]{0:T(256)S(1)} %add_add_fusion.1), channel_id=1, source_target_pairs={{0,128},{16,144},{32,160},{48,176},{64,192},{80,208},{96,224},{112... | collective-permute-start | bytes 3080 | tf_op jit(solution)/shard_map/ppermute | solution.py:45
  36.1 11.0 %collective-permute-start.17 = (f32[256]{0:T(256)S(1)}, f32[256]{0:T(256)S(1)}, u32[]{:S(2)}, u32[]{:S(2)}) collective-permute-start(f32[256]{0:T(256)S(1)} %add_add_fusion.1), channel_id=1, source_target_pairs={{0,192},{16,208},{32,224},{48,240},{64,0},{80,16},{96,32},{112,48}... | collective-permute-start | bytes 3080 | tf_op jit(solution)/shard_map/ppermute | solution.py:45
  40.3 12.1 %collective-permute-start.4 = (f32[12,12,2,256]{3,2,1,0:T(2,128)S(1)}, f32[12,12,2,256]{3,2,1,0:T(2,128)S(1)}, u32[]{:S(2)}, u32[]{:S(2)}) collective-permute-start(f32[12,12,2,256]{3,2,1,0:T(2,128)S(1)} %get-tuple-element.29), channel_id=1, source_target_pairs={{0,1},{1,2},{2,3},{3,0},{4,5},{5,6},{6,7},{7,4},{8,9},{9,10},{10,1... | collective-permute-start | bytes 884744 | tf_op jit(solution)/shard_map/ppermute | solution.py:17
  47.1 8.7 %collective-permute-start.5 = (f32[12,12,2,256]{3,2,1,0:T(2,128)S(1)}, f32[12,12,2,256]{3,2,1,0:T(2,128)S(1)}, u32[]{:S(2)}, u32[]{:S(2)}) collective-permute-start(f32[12,12,2,256]{3,2,1,0:T(2,128)S(1)} %get-tuple-element.28), channel_id=1, source_target_pairs={{1,0},{2,1},{3,2},{0,3},{5,4},{6,5},{7,6},{4,7},{9,8},{10,9},{11,1... | collective-permute-start | bytes 884744 | tf_op jit(solution)/shard_map/ppermute | solution.py:18
  56.9 2.9 %copy-start.1 = (bf16[256,256]{1,0:T(8,128)(2,1)S(1)}, bf16[256,256]{1,0:T(8,128)(2,1)}, u32[]{:S(2)}) copy-start(bf16[256,256]{1,0:T(8,128)(2,1)} %base_ref.1) | copy-start | bytes 393220
  56.9 2.9 %copy-start.2 = (f32[98,256]{1,0:T(8,128)S(1)}, f32[98,256]{1,0:T(8,128)}, u32[]{:S(2)}) copy-start(f32[98,256]{1,0:T(8,128)} %rs_ref.1) | copy-start | bytes 301060
  56.9 2.9 %copy-start.3 = (f32[98,256]{1,0:T(8,128)S(1)}, f32[98,256]{1,0:T(8,128)}, u32[]{:S(2)}) copy-start(f32[98,256]{1,0:T(8,128)} %cs_ref.1) | copy-start | bytes 301060
  56.9 2.9 %copy-start.4 = (s32[294]{0:T(512)S(1)}, s32[294]{0:T(512)}, u32[]{:S(2)}) copy-start(s32[294]{0:T(512)} %constant.59.clone.tab_ref) | copy-start | bytes 3532
  57.3 2.5 %copy-start.5 = (f32[5,12,12,8,256]{4,3,2,1,0:T(8,128)}, f32[5,12,12,8,256]{4,3,2,1,0:T(8,128)S(1)}, u32[]{:S(2)}) copy-start(f32[5,12,12,8,256]{4,3,2,1,0:T(8,128)S(1)} %fusion.8.ysh_ref) | copy-start | bytes 17694724
  82.6 8.0 %collective-permute-start.18 = (bf16[2,8,8,256]{3,2,1,0:T(8,128)(2,1)S(1)}, bf16[2,8,8,256]{3,2,1,0:T(8,128)(2,1)S(1)}, u32[]{:S(2)}, u32[]{:S(2)}) collective-permute-start(bf16[2,8,8,256]{3,2,1,0:T(8,128)(2,1)S(1)} %bitcast.40), channel_id=1, source_target_pairs={{0,16},{16,32},{32,48},{48,64},{64,80},{80,96},{96,112},{112,128},... | collective-permute-start | bytes 196616 | tf_op jit(solution)/shard_map/ppermute | solution.py:17
  85.2 6.1 %collective-permute-start.19 = (bf16[2,8,8,256]{3,2,1,0:T(8,128)(2,1)S(1)}, bf16[2,8,8,256]{3,2,1,0:T(8,128)(2,1)S(1)}, u32[]{:S(2)}, u32[]{:S(2)}) collective-permute-start(bf16[2,8,8,256]{3,2,1,0:T(8,128)(2,1)S(1)} %bitcast.39), channel_id=1, source_target_pairs={{16,0},{32,16},{48,32},{64,48},{80,64},{96,80},{112,96},{128,112},... | collective-permute-start | bytes 196616 | tf_op jit(solution)/shard_map/ppermute | solution.py:18

commit v2 on v1

--- a/solution.py
+++ b/solution.py
@@ -32,19 +32,10 @@
 
 def axis_sum(x, axis):
     count = lax.axis_size(axis)
-    stride = 1
-    while stride < count:
-        group = min(4, count // stride)
-        span = stride * group
-        total = x
-        for k in range(1, group):
-            pairs = []
-            for i in range(count):
-                block, rest = divmod(i, span)
-                pairs.append((i, block * span + (rest + k * stride) % span))
-            total = total + lax.ppermute(x, axis, pairs)
-        x = total
-        stride = span
+    bit = 1
+    while bit < count:
+        x = x + lax.ppermute(x, axis, [(i, i ^ bit) for i in range(count)])
+        bit *= 2
     return x
 
 

time: 96.8 us -> 116 us (1.20)
  the two profiles are of different devices: /device:TPU:6 before, /device:TPU:120 now
where the time goes in v2:
time: 116 us
  waiting for transfers between devices  50.7 us (44%)
  starting transfers between devices  25.6 us (22%)
  Pallas kernels  21.9 us (19%)
  local copies, waits for them, and re-layouts  7.3 us (6%)
  matrix products  6.83 us (6%)
  other arithmetic  2.48 us (2%)
    ppermute x8, waiting for transfers between devices, axis_sum(): x = x + lax.ppermute(x, axis, [(i, i ^ bit) for i in range(count)])  27 us
    pallas_call x1, Pallas kernels, far_field(): pl.pallas_call(far_kernel, out_shape=jax.ShapeDtypeStruct((rows, componen...  21.9 us
    ppermute x8, starting transfers between devices, axis_sum(): x = x + lax.ppermute(x, axis, [(i, i ^ bit) for i in range(count)])  10.7 us
    ppermute x3, starting transfers between devices, padded_2(): before = lax.ppermute(last, axis, up)  7.54 us
    ppermute x3, waiting for transfers between devices, padded_2(): before = lax.ppermute(last, axis, up)  6.28 us
    ppermute x3, waiting for transfers between devices, padded_2(): after = lax.ppermute(leading, axis, down)  6 us
    unnamed x24, local copies, waits for them, and re-layouts  6 us
    ppermute x1, waiting for transfers between devices, per_device(): from_below = lax.ppermute(partial_near[depth:], 'rows', up)  5.75 us
  transfers between devices with their start and end apart: 16, of which 13 were waited for; matrix products, arithmetic and copies ran while one was open for 1% of the time, Pallas kernels for 0%

profile of v2, /device:TPU:120, one launch (start us, length us, event | category | flops | bytes accessed | tf_op | source)
XLA Modules:
  0.0 115.6 jit_solution(1365606342087993485)
XLA Ops:
  0.6 0.0 copy-start
  0.6 0.0 copy-start.7
  0.7 0.0 copy-start.8
  0.7 0.0 copy-start.9
  0.7 3.0 %copy.12 = bf16[4096,256]{0,1:T(8,128)(2,1)S(1)} copy(bf16[4096,256]{1,0:T(8,128)(2,1)} %param.14) | data formatting | bytes 4194304 | tf_op args[0]
  3.6 0.0 copy-done.7
  3.7 0.0 copy-done.8
  3.7 0.0 copy-done.9
  3.7 2.4 %fusion = f32[768,256]{1,0:T(8,128)S(1)} fusion(s32[4096]{0:T(1024)S(1)} %copy-done.9, bf16[4096,256]{0,1:T(8,128)(2,1)S(1)} %copy.12, f32[4096]{0:T(1024)S(1)} %convert_multiply_fusion.1), kind=kOutput, calls=%fused_computation.2 | convolution fusion | flops 1616904192 | bytes 2916352 | tf_op jit(solution)/shard_map/dot_general | solution.py:100
  6.1 3.9 %collective-permute-start = (f32[4,8,8,256]{3,2,1,0:T(8,128)S(1)}, f32[4,8,8,256]{3,2,1,0:T(8,128)S(1)}, u32[]{:S(2)}, u32[]{:S(2)}) collective-permute-start(f32[4,8,8,256]{3,2,1,0:T(8,128)S(1)} %bitcast.38), channel_id=1, source_target_pairs={{0,16},{16,32},{32,48},{48,64},{64,80},{80,96},{96,112},{112,128},... | collective-permute-start | bytes 786440 | tf_op jit(solution)/shard_map/ppermute | solution.py:105
  10.0 0.0 collective-permute-start.1
  10.0 5.8 %collective-permute-done = f32[4,8,8,256]{3,2,1,0:T(8,128)S(1)} collective-permute-done((f32[4,8,8,256]{3,2,1,0:T(8,128)S(1)}, f32[4,8,8,256]{3,2,1,0:T(8,128)S(1)}, u32[]{:S(2)}, u32[]{:S(2)}) %collective-permute-start) | collective-permute-done | bytes 262176 | tf_op jit(solution)/shard_map/ppermute | solution.py:105
  15.8 5.6 %collective-permute-done.1 = f32[4,8,8,256]{3,2,1,0:T(8,128)S(1)} collective-permute-done((f32[4,8,8,256]{3,2,1,0:T(8,128)S(1)}, f32[4,8,8,256]{3,2,1,0:T(8,128)S(1)}, u32[]{:S(2)}, u32[]{:S(2)}) %collective-permute-start.1) | collective-permute-done | bytes 262176 | tf_op jit(solution)/shard_map/ppermute | solution.py:106
  21.4 0.1 fusion.12
  21.5 0.1 collective-permute-start.2
  21.6 0.0 copy-start.6
  21.6 1.7 %collective-permute-start.3 = (f32[12,2,8,256]{3,2,1,0:T(8,128)S(1)}, f32[12,2,8,256]{3,2,1,0:T(8,128)S(1)}, u32[]{:S(2)}, u32[]{:S(2)}) collective-permute-start(f32[12,2,8,256]{3,2,1,0:T(8,128)S(1)} %get-tuple-element.31), channel_id=1, source_target_pairs={{4,0},{8,4},{12,8},{0,12},{5,1},{9,5},{13,9},{1,13},{6,2},{10,6},{... | collective-permute-start | bytes 589832 | tf_op jit(solution)/shard_map/ppermute | solution.py:18
  23.3 4.4 %collective-permute-done.2 = f32[12,2,8,256]{3,2,1,0:T(8,128)S(1)} collective-permute-done((f32[12,2,8,256]{3,2,1,0:T(8,128)S(1)}, f32[12,2,8,256]{3,2,1,0:T(8,128)S(1)}, u32[]{:S(2)}, u32[]{:S(2)}) %collective-permute-start.2) | collective-permute-done | bytes 196640 | tf_op jit(solution)/shard_map/ppermute | solution.py:17
  27.7 0.0 collective-permute-done.3
  27.7 0.1 pad_maximum_fusion.1
  27.8 0.2 fusion.13
  28.0 1.6 %collective-permute-start.4 = (f32[12,12,2,256]{3,2,1,0:T(2,128)S(1)}, f32[12,12,2,256]{3,2,1,0:T(2,128)S(1)}, u32[]{:S(2)}, u32[]{:S(2)}) collective-permute-start(f32[12,12,2,256]{3,2,1,0:T(2,128)S(1)} %get-tuple-element.29), channel_id=1, source_target_pairs={{0,1},{1,2},{2,3},{3,0},{4,5},{5,6},{6,7},{7,4},{8,9},{9,10},{10,1... | collective-permute-start | bytes 884744 | tf_op jit(solution)/shard_map/ppermute | solution.py:17
  29.5 1.8 %collective-permute-start.5 = (f32[12,12,2,256]{3,2,1,0:T(2,128)S(1)}, f32[12,12,2,256]{3,2,1,0:T(2,128)S(1)}, u32[]{:S(2)}, u32[]{:S(2)}) collective-permute-start(f32[12,12,2,256]{3,2,1,0:T(2,128)S(1)} %get-tuple-element.28), channel_id=1, source_target_pairs={{1,0},{2,1},{3,2},{0,3},{5,4},{6,5},{7,6},{4,7},{9,8},{10,9},{11,1... | collective-permute-start | bytes 884744 | tf_op jit(solution)/shard_map/ppermute | solution.py:18
  31.3 0.5 convert_reduce_fusion
  31.8 0.3 collective-permute-start.6
  32.1 7.0 %collective-permute-done.6 = f32[256]{0:T(256)S(1)} collective-permute-done((f32[256]{0:T(256)S(1)}, f32[256]{0:T(256)S(1)}, u32[]{:S(2)}, u32[]{:S(2)}) %collective-permute-start.6) | collective-permute-done | bytes 1056 | tf_op jit(solution)/shard_map/ppermute | solution.py:37
  39.1 2.7 %collective-permute-start.7 = (f32[256]{0:T(256)S(1)}, f32[256]{0:T(256)S(1)}, u32[]{:S(2)}, u32[]{:S(2)}) collective-permute-start(f32[256]{0:T(256)S(1)} %add.40), channel_id=1, source_target_pairs={{0,2},{1,3},{2,0},{3,1},{4,6},{5,7},{6,4},{7,5},{8,10},{9,11},{10,... | collective-permute-start | bytes 3080 | tf_op jit(solution)/shard_map/ppermute | solution.py:37
  41.9 2.3 %collective-permute-done.7 = f32[256]{0:T(256)S(1)} collective-permute-done((f32[256]{0:T(256)S(1)}, f32[256]{0:T(256)S(1)}, u32[]{:S(2)}, u32[]{:S(2)}) %collective-permute-start.7) | collective-permute-done | bytes 1056 | tf_op jit(solution)/shard_map/ppermute | solution.py:37
  44.2 0.0 collective-permute-start.8
  44.2 1.2 %collective-permute-done.8 = f32[256]{0:T(256)S(1)} collective-permute-done((f32[256]{0:T(256)S(1)}, f32[256]{0:T(256)S(1)}, u32[]{:S(2)}, u32[]{:S(2)}) %collective-permute-start.8) | collective-permute-done | bytes 1056 | tf_op jit(solution)/shard_map/ppermute | solution.py:37
  45.4 0.8 collective-permute-start.9
  46.2 2.8 %collective-permute-done.9 = f32[256]{0:T(256)S(1)} collective-permute-done((f32[256]{0:T(256)S(1)}, f32[256]{0:T(256)S(1)}, u32[]{:S(2)}, u32[]{:S(2)}) %collective-permute-start.9) | collective-permute-done | bytes 1056 | tf_op jit(solution)/shard_map/ppermute | solution.py:37
  48.9 2.1 %collective-permute-start.10 = (f32[256]{0:T(256)S(1)}, f32[256]{0:T(256)S(1)}, u32[]{:S(2)}, u32[]{:S(2)}) collective-permute-start(f32[256]{0:T(256)S(1)} %add.43), channel_id=1, source_target_pairs={{0,16},{16,0},{32,48},{48,32},{64,80},{80,64},{96,112},{112,96},{1... | collective-permute-start | bytes 3080 | tf_op jit(solution)/shard_map/ppermute | solution.py:37
  51.1 2.9 %collective-permute-done.10 = f32[256]{0:T(256)S(1)} collective-permute-done((f32[256]{0:T(256)S(1)}, f32[256]{0:T(256)S(1)}, u32[]{:S(2)}, u32[]{:S(2)}) %collective-permute-start.10) | collective-permute-done | bytes 1056 | tf_op jit(solution)/shard_map/ppermute | solution.py:37
  54.0 0.1 collective-permute-start.11
  54.2 3.4 %collective-permute-done.11 = f32[256]{0:T(256)S(1)} collective-permute-done((f32[256]{0:T(256)S(1)}, f32[256]{0:T(256)S(1)}, u32[]{:S(2)}, u32[]{:S(2)}) %collective-permute-start.11) | collective-permute-done | bytes 1056 | tf_op jit(solution)/shard_map/ppermute | solution.py:37
  57.6 0.0 collective-permute-start.12
  57.6 4.5 %collective-permute-done.12 = f32[256]{0:T(256)S(1)} collective-permute-done((f32[256]{0:T(256)S(1)}, f32[256]{0:T(256)S(1)}, u32[]{:S(2)}, u32[]{:S(2)}) %collective-permute-start.12) | collective-permute-done | bytes 1056 | tf_op jit(solution)/shard_map/ppermute | solution.py:37
  62.1 4.5 %collective-permute-start.13 = (f32[256]{0:T(256)S(1)}, f32[256]{0:T(256)S(1)}, u32[]{:S(2)}, u32[]{:S(2)}) collective-permute-start(f32[256]{0:T(256)S(1)} %add.46), channel_id=1, source_target_pairs={{0,128},{16,144},{32,160},{48,176},{64,192},{80,208},{96,224},{112... | collective-permute-start | bytes 3080 | tf_op jit(solution)/shard_map/ppermute | solution.py:37
  66.6 0.0 copy-done.6
  66.6 2.9 %collective-permute-done.13 = f32[256]{0:T(256)S(1)} collective-permute-done((f32[256]{0:T(256)S(1)}, f32[256]{0:T(256)S(1)}, u32[]{:S(2)}, u32[]{:S(2)}) %collective-permute-start.13) | collective-permute-done | bytes 1056 | tf_op jit(solution)/shard_map/ppermute | solution.py:37
  69.6 0.2 fusion.17.lat_ref
  69.8 0.0 collective-permute-done.4
  69.8 0.0 collective-permute-done.5
  69.8 0.7 pad_maximum_fusion
  70.5 0.1 fusion.11
  70.6 0.2 fusion.10
  70.8 0.1 bitcast_dynamic-update-slice_fusion
  70.9 0.0 copy-start.1
  70.9 0.0 copy-start.2
  70.9 0.0 copy-start.3
  70.9 0.0 copy-start.4
  70.9 0.2 fusion.9
  71.1 0.2 fusion.8.ysh_ref
  71.3 2.5 %copy-done.5 = f32[5,12,12,8,256]{4,3,2,1,0:T(8,128)} copy-done((f32[5,12,12,8,256]{4,3,2,1,0:T(8,128)}, f32[5,12,12,8,256]{4,3,2,1,0:T(8,128)S(1)}, u32[]{:S(2)}) %copy-start.5) | copy-done | bytes 5898264
  73.8 0.0 copy-done.3
  73.8 21.9 %shard_map.113 = bf16[512,256]{1,0:T(8,128)(2,1)} custom-call(s32[294]{0:T(512)S(1)} %copy-done.4, f32[5,12,12,8,256]{4,3,2,1,0:T(8,128)} %copy-done.5, f32[512,98]{1,0:T(8,128)S(1)} %bitcast.31, f32[98,256]{1,0:T(8,128)S(1)} %copy-done.2, f32[98,256]{1,0:T(8,128)S(1)} %copy-done.3, bf16[256,256]{1,0:T(8,128)(2,1)S(1)} %copy-done.1, f32[1,256]{1,0:T(1,128)S(1)} %fusion.17.lat_ref), custom_call_target="tpu_custom_call" | custom-call | tf_op jit(solution)/shard_map/pallas_call | solution.py:76
  95.7 0.9 fusion.16
  96.6 5.9 %collective-permute-start.14 = (bf16[2,8,8,256]{3,2,1,0:T(8,128)(2,1)S(1)}, bf16[2,8,8,256]{3,2,1,0:T(8,128)(2,1)S(1)}, u32[]{:S(2)}, u32[]{:S(2)}) collective-permute-start(bf16[2,8,8,256]{3,2,1,0:T(8,128)(2,1)S(1)} %bitcast.40), channel_id=1, source_target_pairs={{0,16},{16,32},{32,48},{48,64},{64,80},{80,96},{96,112},{112,128},... | collective-permute-start | bytes 196616 | tf_op jit(solution)/shard_map/ppermute | solution.py:17
  102.5 0.0 collective-permute-start.15
  102.5 1.9 %collective-permute-done.14 = bf16[2,8,8,256]{3,2,1,0:T(8,128)(2,1)S(1)} collective-permute-done((bf16[2,8,8,256]{3,2,1,0:T(8,128)(2,1)S(1)}, bf16[2,8,8,256]{3,2,1,0:T(8,128)(2,1)S(1)}, u32[]{:S(2)}, u32[]{:S(2)}) %collective-permute-start.14) | collective-permute-done | bytes 65568 | tf_op jit(solution)/shard_map/ppermute | solution.py:17
  104.4 6.0 %collective-permute-done.15 = bf16[2,8,8,256]{3,2,1,0:T(8,128)(2,1)S(1)} collective-permute-done((bf16[2,8,8,256]{3,2,1,0:T(8,128)(2,1)S(1)}, bf16[2,8,8,256]{3,2,1,0:T(8,128)(2,1)S(1)}, u32[]{:S(2)}, u32[]{:S(2)}) %collective-permute-start.15) | collective-permute-done | bytes 65568 | tf_op jit(solution)/shard_map/ppermute | solution.py:18
  110.4 1.0 pad_maximum_fusion.2
  111.4 4.3 %fusion.7 = f32[4096]{0:T(1024)} fusion(bf16[768,256]{1,0:T(8,128)(2,1)S(1)} %bitcast.37, s32[4096]{0:T(1024)S(1)} %copy-done.9, bf16[4096,256]{0,1:T(8,128)(2,1)S(1)} %copy.12), kind=kOutput, calls=%fused_computation.12 | convolution fusion | flops 1616900096 | bytes 2523136 | tf_op jit(solution)/shard_map/dot_general | solution.py:116
  (18 shorter events, 0.2 us)
Async XLA Ops:
  0.6 68.9 %copy-start = (f32[256,256]{1,0:T(8,128)S(1)}, f32[256,256]{1,0:T(8,128)}, u32[]{:S(2)}) copy-start(f32[256,256]{1,0:T(8,128)} %param.22) | copy-start | bytes 786436
  0.6 3.0 %copy-start.7 = (f32[4096]{0:T(1024)S(1)}, f32[4096]{0:T(1024)}, u32[]{:S(2)}) copy-start(f32[4096]{0:T(1024)} %param.15) | copy-start | bytes 49156
  0.7 3.0 %copy-start.8 = (s32[4096]{0:T(1024)S(1)}, s32[4096]{0:T(1024)}, u32[]{:S(2)}) copy-start(s32[4096]{0:T(1024)} %param.16) | copy-start | bytes 49156
  0.7 3.0 %copy-start.9 = (s32[4096]{0:T(1024)S(1)}, s32[4096]{0:T(1024)}, u32[]{:S(2)}) copy-start(s32[4096]{0:T(1024)} %param.17) | copy-start | bytes 49156
  6.1 9.6 %collective-permute-start = (f32[4,8,8,256]{3,2,1,0:T(8,128)S(1)}, f32[4,8,8,256]{3,2,1,0:T(8,128)S(1)}, u32[]{:S(2)}, u32[]{:S(2)}) collective-permute-start(f32[4,8,8,256]{3,2,1,0:T(8,128)S(1)} %bitcast.38), channel_id=1, source_target_pairs={{0,16},{16,32},{32,48},{48,64},{64,80},{80,96},{96,112},{112,128},... | collective-permute-start | bytes 786440 | tf_op jit(solution)/shard_map/ppermute | solution.py:105
  10.0 11.4 %collective-permute-start.1 = (f32[4,8,8,256]{3,2,1,0:T(8,128)S(1)}, f32[4,8,8,256]{3,2,1,0:T(8,128)S(1)}, u32[]{:S(2)}, u32[]{:S(2)}) collective-permute-start(f32[4,8,8,256]{3,2,1,0:T(8,128)S(1)} %bitcast.35), channel_id=1, source_target_pairs={{16,0},{32,16},{48,32},{64,48},{80,64},{96,80},{112,96},{128,112},... | collective-permute-start | bytes 786440 | tf_op jit(solution)/shard_map/ppermute | solution.py:106
  21.5 6.2 %collective-permute-start.2 = (f32[12,2,8,256]{3,2,1,0:T(8,128)S(1)}, f32[12,2,8,256]{3,2,1,0:T(8,128)S(1)}, u32[]{:S(2)}, u32[]{:S(2)}) collective-permute-start(f32[12,2,8,256]{3,2,1,0:T(8,128)S(1)} %get-tuple-element.30), channel_id=1, source_target_pairs={{0,4},{4,8},{8,12},{12,0},{1,5},{5,9},{9,13},{13,1},{2,6},{6,10},{... | collective-permute-start | bytes 589832 | tf_op jit(solution)/shard_map/ppermute | solution.py:17
  21.6 45.0 %copy-start.6 = (s32[8,8,8,98]{3,2,1,0:T(8,128)S(1)}, s32[8,8,8,98]{3,2,1,0:T(8,128)}, u32[]{:S(2)}) copy-start(s32[8,8,8,98]{3,2,1,0:T(8,128)} %param.18) | copy-start | bytes 602116
  21.6 6.1 %collective-permute-start.3 = (f32[12,2,8,256]{3,2,1,0:T(8,128)S(1)}, f32[12,2,8,256]{3,2,1,0:T(8,128)S(1)}, u32[]{:S(2)}, u32[]{:S(2)}) collective-permute-start(f32[12,2,8,256]{3,2,1,0:T(8,128)S(1)} %get-tuple-element.31), channel_id=1, source_target_pairs={{4,0},{8,4},{12,8},{0,12},{5,1},{9,5},{13,9},{1,13},{6,2},{10,6},{... | collective-permute-start | bytes 589832 | tf_op jit(solution)/shard_map/ppermute | solution.py:18
  28.0 41.8 %collective-permute-start.4 = (f32[12,12,2,256]{3,2,1,0:T(2,128)S(1)}, f32[12,12,2,256]{3,2,1,0:T(2,128)S(1)}, u32[]{:S(2)}, u32[]{:S(2)}) collective-permute-start(f32[12,12,2,256]{3,2,1,0:T(2,128)S(1)} %get-tuple-element.29), channel_id=1, source_target_pairs={{0,1},{1,2},{2,3},{3,0},{4,5},{5,6},{6,7},{7,4},{8,9},{9,10},{10,1... | collective-permute-start | bytes 884744 | tf_op jit(solution)/shard_map/ppermute | solution.py:17
  29.5 40.3 %collective-permute-start.5 = (f32[12,12,2,256]{3,2,1,0:T(2,128)S(1)}, f32[12,12,2,256]{3,2,1,0:T(2,128)S(1)}, u32[]{:S(2)}, u32[]{:S(2)}) collective-permute-start(f32[12,12,2,256]{3,2,1,0:T(2,128)S(1)} %get-tuple-element.28), channel_id=1, source_target_pairs={{1,0},{2,1},{3,2},{0,3},{5,4},{6,5},{7,6},{4,7},{9,8},{10,9},{11,1... | collective-permute-start | bytes 884744 | tf_op jit(solution)/shard_map/ppermute | solution.py:18
  31.8 7.3 %collective-permute-start.6 = (f32[256]{0:T(256)S(1)}, f32[256]{0:T(256)S(1)}, u32[]{:S(2)}, u32[]{:S(2)}) collective-permute-start(f32[256]{0:T(256)S(1)} %convert_reduce_fusion), channel_id=1, source_target_pairs={{0,1},{1,0},{2,3},{3,2},{4,5},{5,4},{6,7},{7,6},{8,9},{9,8},{10,11... | collective-permute-start | bytes 3080 | tf_op jit(solution)/shard_map/ppermute | solution.py:37
  39.1 5.1 %collective-permute-start.7 = (f32[256]{0:T(256)S(1)}, f32[256]{0:T(256)S(1)}, u32[]{:S(2)}, u32[]{:S(2)}) collective-permute-start(f32[256]{0:T(256)S(1)} %add.40), channel_id=1, source_target_pairs={{0,2},{1,3},{2,0},{3,1},{4,6},{5,7},{6,4},{7,5},{8,10},{9,11},{10,... | collective-permute-start | bytes 3080 | tf_op jit(solution)/shard_map/ppermute | solution.py:37
  44.2 1.2 %collective-permute-start.8 = (f32[256]{0:T(256)S(1)}, f32[256]{0:T(256)S(1)}, u32[]{:S(2)}, u32[]{:S(2)}) collective-permute-start(f32[256]{0:T(256)S(1)} %add.41), channel_id=1, source_target_pairs={{0,4},{4,0},{8,12},{12,8},{1,5},{5,1},{9,13},{13,9},{2,6},{6,2},{1... | collective-permute-start | bytes 3080 | tf_op jit(solution)/shard_map/ppermute | solution.py:37
  45.4 3.6 %collective-permute-start.9 = (f32[256]{0:T(256)S(1)}, f32[256]{0:T(256)S(1)}, u32[]{:S(2)}, u32[]{:S(2)}) collective-permute-start(f32[256]{0:T(256)S(1)} %add.42), channel_id=1, source_target_pairs={{0,8},{4,12},{8,0},{12,4},{1,9},{5,13},{9,1},{13,5},{2,10},{6,14},... | collective-permute-start | bytes 3080 | tf_op jit(solution)/shard_map/ppermute | solution.py:37
  48.9 5.1 %collective-permute-start.10 = (f32[256]{0:T(256)S(1)}, f32[256]{0:T(256)S(1)}, u32[]{:S(2)}, u32[]{:S(2)}) collective-permute-start(f32[256]{0:T(256)S(1)} %add.43), channel_id=1, source_target_pairs={{0,16},{16,0},{32,48},{48,32},{64,80},{80,64},{96,112},{112,96},{1... | collective-permute-start | bytes 3080 | tf_op jit(solution)/shard_map/ppermute | solution.py:37
  54.0 3.6 %collective-permute-start.11 = (f32[256]{0:T(256)S(1)}, f32[256]{0:T(256)S(1)}, u32[]{:S(2)}, u32[]{:S(2)}) collective-permute-start(f32[256]{0:T(256)S(1)} %add.44), channel_id=1, source_target_pairs={{0,32},{16,48},{32,0},{48,16},{64,96},{80,112},{96,64},{112,80},{1... | collective-permute-start | bytes 3080 | tf_op jit(solution)/shard_map/ppermute | solution.py:37
  57.6 4.5 %collective-permute-start.12 = (f32[256]{0:T(256)S(1)}, f32[256]{0:T(256)S(1)}, u32[]{:S(2)}, u32[]{:S(2)}) collective-permute-start(f32[256]{0:T(256)S(1)} %add.45), channel_id=1, source_target_pairs={{0,64},{16,80},{32,96},{48,112},{64,0},{80,16},{96,32},{112,48},{1... | collective-permute-start | bytes 3080 | tf_op jit(solution)/shard_map/ppermute | solution.py:37
  62.1 7.5 %collective-permute-start.13 = (f32[256]{0:T(256)S(1)}, f32[256]{0:T(256)S(1)}, u32[]{:S(2)}, u32[]{:S(2)}) collective-permute-start(f32[256]{0:T(256)S(1)} %add.46), channel_id=1, source_target_pairs={{0,128},{16,144},{32,160},{48,176},{64,192},{80,208},{96,224},{112... | collective-permute-start | bytes 3080 | tf_op jit(solution)/shard_map/ppermute | solution.py:37
  70.9 2.9 %copy-start.1 = (bf16[256,256]{1,0:T(8,128)(2,1)S(1)}, bf16[256,256]{1,0:T(8,128)(2,1)}, u32[]{:S(2)}) copy-start(bf16[256,256]{1,0:T(8,128)(2,1)} %base_ref.1) | copy-start | bytes 393220
  70.9 2.9 %copy-start.2 = (f32[98,256]{1,0:T(8,128)S(1)}, f32[98,256]{1,0:T(8,128)}, u32[]{:S(2)}) copy-start(f32[98,256]{1,0:T(8,128)} %rs_ref.1) | copy-start | bytes 301060
  70.9 2.9 %copy-start.3 = (f32[98,256]{1,0:T(8,128)S(1)}, f32[98,256]{1,0:T(8,128)}, u32[]{:S(2)}) copy-start(f32[98,256]{1,0:T(8,128)} %cs_ref.1) | copy-start | bytes 301060
  70.9 2.9 %copy-start.4 = (s32[294]{0:T(512)S(1)}, s32[294]{0:T(512)}, u32[]{:S(2)}) copy-start(s32[294]{0:T(512)} %constant.59.clone.tab_ref) | copy-start | bytes 3532
  71.3 2.5 %copy-start.5 = (f32[5,12,12,8,256]{4,3,2,1,0:T(8,128)}, f32[5,12,12,8,256]{4,3,2,1,0:T(8,128)S(1)}, u32[]{:S(2)}) copy-start(f32[5,12,12,8,256]{4,3,2,1,0:T(8,128)S(1)} %fusion.8.ysh_ref) | copy-start | bytes 17694724
  96.6 7.8 %collective-permute-start.14 = (bf16[2,8,8,256]{3,2,1,0:T(8,128)(2,1)S(1)}, bf16[2,8,8,256]{3,2,1,0:T(8,128)(2,1)S(1)}, u32[]{:S(2)}, u32[]{:S(2)}) collective-permute-start(bf16[2,8,8,256]{3,2,1,0:T(8,128)(2,1)S(1)} %bitcast.40), channel_id=1, source_target_pairs={{0,16},{16,32},{32,48},{48,64},{64,80},{80,96},{96,112},{112,128},... | collective-permute-start | bytes 196616 | tf_op jit(solution)/shard_map/ppermute | solution.py:17
  102.5 7.9 %collective-permute-start.15 = (bf16[2,8,8,256]{3,2,1,0:T(8,128)(2,1)S(1)}, bf16[2,8,8,256]{3,2,1,0:T(8,128)(2,1)S(1)}, u32[]{:S(2)}, u32[]{:S(2)}) collective-permute-start(bf16[2,8,8,256]{3,2,1,0:T(8,128)(2,1)S(1)} %bitcast.39), channel_id=1, source_target_pairs={{16,0},{32,16},{48,32},{64,48},{80,64},{96,80},{112,96},{128,112},... | collective-permute-start | bytes 196616 | tf_op jit(solution)/shard_map/ppermute | solution.py:18

commit v3 on v1

--- a/solution.py
+++ b/solution.py
@@ -104,6 +104,7 @@
     cell_part = jnp.sum(weighted.astype(jnp.float32), 0)
     cell = axis_sum(axis_sum(axis_sum(cell_part, "by"), "bx"), "rows")
     lattice_term = jnp.dot(cell, lattice, precision=lax.Precision.HIGHEST)
+    weighted, lattice_term = lax.optimization_barrier((weighted, lattice_term))
     labels = lax.iota(jnp.int32, near_boxes)
     selector = (labels[:, None] == pair_box[None, :]).astype(jnp.bfloat16)
     partial_near = jnp.dot(selector, weighted, preferred_element_type=jnp.float32)

time: 96.8 us -> 115 us (1.19)
  waiting for transfers between devices: 14.2 us -> 36.8 us
  starting transfers between devices: 42.9 us -> 37.4 us
    ppermute x12, waiting for transfers between devices: 0.03 us -> 12.7 us  [axis_sum(): total = total + lax.ppermute(x, axis, pairs)]
    ppermute x3, starting transfers between devices: 9.74 us -> 1.53 us  [padded_2(): before = lax.ppermute(last, axis, up)]
    ppermute x3, waiting for transfers between devices: 7.36 us -> 13.4 us  [padded_2(): before = lax.ppermute(last, axis, up)]
    ppermute x1, waiting for transfers between devices: 0.01 us -> 4.61 us  [per_device(): from_below = lax.ppermute(partial_near[depth:], 'rows', up)]
    ppermute x12, starting transfers between devices: 17.3 us -> 21.8 us  [axis_sum(): total = total + lax.ppermute(x, axis, pairs)]
    ppermute x1, starting transfers between devices: 8.06 us -> 4.22 us  [per_device(): from_above = lax.ppermute(partial_near[:4], 'rows', down)]
    ppermute x3, starting transfers between devices: 4.81 us -> 8.1 us  [padded_2(): after = lax.ppermute(leading, axis, down)]
    ppermute x3, waiting for transfers between devices: 4.08 us -> 2.5 us  [padded_2(): after = lax.ppermute(leading, axis, down)]
  transfers between devices with their start and end apart: 20 -> 20, of which waited for: 5 -> 16; matrix products, arithmetic and copies ran while one was open for 3% -> 0% of each run, Pallas kernels for 0% -> 0%
where the time goes in v3:
time: 115 us; the launch traced here: 114 us
  starting transfers between devices  37.4 us (33%)
  waiting for transfers between devices  36.8 us (32%)
  Pallas kernels  22.1 us (19%)
  local copies, waits for them, and re-layouts  7.31 us (6%)
  matrix products  6.79 us (6%)
  other arithmetic  2.75 us (2%)
    pallas_call x1, Pallas kernels, far_field(): pl.pallas_call(far_kernel, out_shape=jax.ShapeDtypeStruct((rows, componen...  22.1 us
    ppermute x12, starting transfers between devices, axis_sum(): total = total + lax.ppermute(x, axis, pairs)  21.8 us
    ppermute x3, waiting for transfers between devices, padded_2(): before = lax.ppermute(last, axis, up)  13.4 us
    ppermute x12, waiting for transfers between devices, axis_sum(): total = total + lax.ppermute(x, axis, pairs)  12.7 us
    ppermute x3, starting transfers between devices, padded_2(): after = lax.ppermute(leading, axis, down)  8.1 us
    unnamed x24, local copies, waits for them, and re-layouts  6.01 us
    ppermute x1, waiting for transfers between devices, per_device(): from_below = lax.ppermute(partial_near[depth:], 'rows', up)  4.61 us
    dot_general x1, matrix products, per_device(): jnp.dot(onehot, flat_locals, preferred_element_type=jnp.float32)  4.32 us
  transfers between devices with their start and end apart: 20, of which 16 were waited for; matrix products, arithmetic and copies ran while one was open for 0% of the time, Pallas kernels for 0%

profile of v3, /device:TPU:6, one launch (start us, length us, event | category | flops | bytes accessed | tf_op | source)
XLA Modules:
  0.0 114.0 jit_solution(10382505997892572428)
XLA Ops:
  0.6 0.0 copy-start
  0.7 3.0 %copy.12 = bf16[4096,256]{0,1:T(8,128)(2,1)S(1)} copy(bf16[4096,256]{1,0:T(8,128)(2,1)} %param.14) | data formatting | bytes 4194304 | tf_op args[0]
  3.6 0.0 copy-start.9
  3.7 0.7 convert_reduce_fusion
  4.4 2.3 %collective-permute-start = (f32[256]{0:T(256)S(1)}, f32[256]{0:T(256)S(1)}, u32[]{:S(2)}, u32[]{:S(2)}) collective-permute-start(f32[256]{0:T(256)S(1)} %get-tuple-element.30), channel_id=1, source_target_pairs={{0,1},{1,2},{2,3},{3,0},{4,5},{5,6},{6,7},{7,4},{8,9},{9,10},{10,1... | collective-permute-start | bytes 3080 | tf_op jit(solution)/shard_map/ppermute | solution.py:45
  6.7 0.7 collective-permute-start.1
  7.4 0.2 collective-permute-start.2
  7.6 0.4 collective-permute-done
  8.0 3.7 %collective-permute-done.1 = f32[256]{0:T(256)S(1)} collective-permute-done((f32[256]{0:T(256)S(1)}, f32[256]{0:T(256)S(1)}, u32[]{:S(2)}, u32[]{:S(2)}) %collective-permute-start.1) | collective-permute-done | bytes 1056 | tf_op jit(solution)/shard_map/ppermute | solution.py:45
  11.7 0.4 collective-permute-done.2
  12.2 1.7 %collective-permute-start.4 = (f32[256]{0:T(256)S(1)}, f32[256]{0:T(256)S(1)}, u32[]{:S(2)}, u32[]{:S(2)}) collective-permute-start(f32[256]{0:T(256)S(1)} %add_add_fusion.3), channel_id=1, source_target_pairs={{0,8},{4,12},{8,0},{12,4},{1,9},{5,13},{9,1},{13,5},{2,10},{6,14},... | collective-permute-start | bytes 3080 | tf_op jit(solution)/shard_map/ppermute | solution.py:45
  13.8 1.4 %collective-permute-start.5 = (f32[256]{0:T(256)S(1)}, f32[256]{0:T(256)S(1)}, u32[]{:S(2)}, u32[]{:S(2)}) collective-permute-start(f32[256]{0:T(256)S(1)} %add_add_fusion.3), channel_id=1, source_target_pairs={{0,12},{4,0},{8,4},{12,8},{1,13},{5,1},{9,5},{13,9},{2,14},{6,2},{... | collective-permute-start | bytes 3080 | tf_op jit(solution)/shard_map/ppermute | solution.py:45
  15.2 0.0 collective-permute-done.3
  15.2 0.6 collective-permute-done.4
  15.8 0.7 collective-permute-done.5
  16.5 2.9 %collective-permute-start.6 = (f32[256]{0:T(256)S(1)}, f32[256]{0:T(256)S(1)}, u32[]{:S(2)}, u32[]{:S(2)}) collective-permute-start(f32[256]{0:T(256)S(1)} %add_add_fusion.2), channel_id=1, source_target_pairs={{0,16},{16,32},{32,48},{48,0},{64,80},{80,96},{96,112},{112,64},{1... | collective-permute-start | bytes 3080 | tf_op jit(solution)/shard_map/ppermute | solution.py:45
  19.4 1.9 %collective-permute-start.7 = (f32[256]{0:T(256)S(1)}, f32[256]{0:T(256)S(1)}, u32[]{:S(2)}, u32[]{:S(2)}) collective-permute-start(f32[256]{0:T(256)S(1)} %add_add_fusion.2), channel_id=1, source_target_pairs={{0,32},{16,48},{32,0},{48,16},{64,96},{80,112},{96,64},{112,80},{1... | collective-permute-start | bytes 3080 | tf_op jit(solution)/shard_map/ppermute | solution.py:45
  21.3 1.5 %collective-permute-start.8 = (f32[256]{0:T(256)S(1)}, f32[256]{0:T(256)S(1)}, u32[]{:S(2)}, u32[]{:S(2)}) collective-permute-start(f32[256]{0:T(256)S(1)} %add_add_fusion.2), channel_id=1, source_target_pairs={{0,48},{16,0},{32,16},{48,32},{64,112},{80,64},{96,80},{112,96},{1... | collective-permute-start | bytes 3080 | tf_op jit(solution)/shard_map/ppermute | solution.py:45
  22.9 0.0 collective-permute-done.6
  22.9 0.1 collective-permute-done.7
  23.0 3.4 %collective-permute-done.8 = f32[256]{0:T(256)S(1)} collective-permute-done((f32[256]{0:T(256)S(1)}, f32[256]{0:T(256)S(1)}, u32[]{:S(2)}, u32[]{:S(2)}) %collective-permute-start.8) | collective-permute-done | bytes 1056 | tf_op jit(solution)/shard_map/ppermute | solution.py:45
  26.4 6.3 %collective-permute-start.10 = (f32[256]{0:T(256)S(1)}, f32[256]{0:T(256)S(1)}, u32[]{:S(2)}, u32[]{:S(2)}) collective-permute-start(f32[256]{0:T(256)S(1)} %add_add_fusion.1), channel_id=1, source_target_pairs={{0,128},{16,144},{32,160},{48,176},{64,192},{80,208},{96,224},{112... | collective-permute-start | bytes 3080 | tf_op jit(solution)/shard_map/ppermute | solution.py:45
  32.7 0.6 collective-permute-start.11
  33.3 2.4 %collective-permute-start.9 = (f32[256]{0:T(256)S(1)}, f32[256]{0:T(256)S(1)}, u32[]{:S(2)}, u32[]{:S(2)}) collective-permute-start(f32[256]{0:T(256)S(1)} %add_add_fusion.1), channel_id=1, source_target_pairs={{0,64},{16,80},{32,96},{48,112},{64,128},{80,144},{96,160},{112,17... | collective-permute-start | bytes 3080 | tf_op jit(solution)/shard_map/ppermute | solution.py:45
  35.6 0.0 collective-permute-done.10
  35.6 1.5 %collective-permute-done.11 = f32[256]{0:T(256)S(1)} collective-permute-done((f32[256]{0:T(256)S(1)}, f32[256]{0:T(256)S(1)}, u32[]{:S(2)}, u32[]{:S(2)}) %collective-permute-start.11) | collective-permute-done | bytes 1056 | tf_op jit(solution)/shard_map/ppermute | solution.py:45
  37.2 1.8 %collective-permute-done.9 = f32[256]{0:T(256)S(1)} collective-permute-done((f32[256]{0:T(256)S(1)}, f32[256]{0:T(256)S(1)}, u32[]{:S(2)}, u32[]{:S(2)}) %collective-permute-start.9) | collective-permute-done | bytes 1056 | tf_op jit(solution)/shard_map/ppermute | solution.py:45
  39.0 0.2 fusion.17
  39.1 2.3 %fusion = f32[768,256]{1,0:T(8,128)S(1)} fusion(bf16[4096,256]{0,1:T(8,128)(2,1)S(1)} %get-tuple-element.28, s32[4096]{0:T(1024)S(1)} %copy-done.9), kind=kOutput, calls=%fused_computation.2 | convolution fusion | flops 1613758464 | bytes 2899968 | tf_op jit(solution)/shard_map/dot_general | solution.py:110
  41.5 1.7 %collective-permute-start.12 = (f32[4,8,8,256]{3,2,1,0:T(8,128)S(1)}, f32[4,8,8,256]{3,2,1,0:T(8,128)S(1)}, u32[]{:S(2)}, u32[]{:S(2)}) collective-permute-start(f32[4,8,8,256]{3,2,1,0:T(8,128)S(1)} %bitcast.40), channel_id=1, source_target_pairs={{0,16},{16,32},{32,48},{48,64},{64,80},{80,96},{96,112},{112,128},... | collective-permute-start | bytes 786440 | tf_op jit(solution)/shard_map/ppermute | solution.py:115
  43.2 4.2 %collective-permute-start.13 = (f32[4,8,8,256]{3,2,1,0:T(8,128)S(1)}, f32[4,8,8,256]{3,2,1,0:T(8,128)S(1)}, u32[]{:S(2)}, u32[]{:S(2)}) collective-permute-start(f32[4,8,8,256]{3,2,1,0:T(8,128)S(1)} %bitcast.37), channel_id=1, source_target_pairs={{16,0},{32,16},{48,32},{64,48},{80,64},{96,80},{112,96},{128,112},... | collective-permute-start | bytes 786440 | tf_op jit(solution)/shard_map/ppermute | solution.py:116
  47.4 4.6 %collective-permute-done.12 = f32[4,8,8,256]{3,2,1,0:T(8,128)S(1)} collective-permute-done((f32[4,8,8,256]{3,2,1,0:T(8,128)S(1)}, f32[4,8,8,256]{3,2,1,0:T(8,128)S(1)}, u32[]{:S(2)}, u32[]{:S(2)}) %collective-permute-start.12) | collective-permute-done | bytes 262176 | tf_op jit(solution)/shard_map/ppermute | solution.py:115
  52.0 3.6 %collective-permute-done.13 = f32[4,8,8,256]{3,2,1,0:T(8,128)S(1)} collective-permute-done((f32[4,8,8,256]{3,2,1,0:T(8,128)S(1)}, f32[4,8,8,256]{3,2,1,0:T(8,128)S(1)}, u32[]{:S(2)}, u32[]{:S(2)}) %collective-permute-start.13) | collective-permute-done | bytes 262176 | tf_op jit(solution)/shard_map/ppermute | solution.py:116
  55.6 0.1 fusion.11
  55.7 0.0 copy-start.6
  55.7 0.1 collective-permute-start.14
  55.8 1.7 %collective-permute-start.15 = (f32[12,2,8,256]{3,2,1,0:T(8,128)S(1)}, f32[12,2,8,256]{3,2,1,0:T(8,128)S(1)}, u32[]{:S(2)}, u32[]{:S(2)}) collective-permute-start(f32[12,2,8,256]{3,2,1,0:T(8,128)S(1)} %get-tuple-element.37), channel_id=1, source_target_pairs={{4,0},{8,4},{12,8},{0,12},{5,1},{9,5},{13,9},{1,13},{6,2},{10,6},{... | collective-permute-start | bytes 589832 | tf_op jit(solution)/shard_map/ppermute | solution.py:18
  57.5 3.6 %collective-permute-done.14 = f32[12,2,8,256]{3,2,1,0:T(8,128)S(1)} collective-permute-done((f32[12,2,8,256]{3,2,1,0:T(8,128)S(1)}, f32[12,2,8,256]{3,2,1,0:T(8,128)S(1)}, u32[]{:S(2)}, u32[]{:S(2)}) %collective-permute-start.14) | collective-permute-done | bytes 196640 | tf_op jit(solution)/shard_map/ppermute | solution.py:17
  61.1 1.0 collective-permute-done.15
  62.1 0.1 pad_maximum_fusion.1
  62.2 0.2 fusion.13
  62.4 0.7 collective-permute-start.16
  63.1 1.4 %collective-permute-start.17 = (f32[12,12,2,256]{3,2,1,0:T(2,128)S(1)}, f32[12,12,2,256]{3,2,1,0:T(2,128)S(1)}, u32[]{:S(2)}, u32[]{:S(2)}) collective-permute-start(f32[12,12,2,256]{3,2,1,0:T(2,128)S(1)} %get-tuple-element.34), channel_id=1, source_target_pairs={{1,0},{2,1},{3,2},{0,3},{5,4},{6,5},{7,6},{4,7},{9,8},{10,9},{11,1... | collective-permute-start | bytes 884744 | tf_op jit(solution)/shard_map/ppermute | solution.py:18
  64.5 7.6 %collective-permute-done.16 = f32[12,12,2,256]{3,2,1,0:T(2,128)S(1)} collective-permute-done((f32[12,12,2,256]{3,2,1,0:T(2,128)S(1)}, f32[12,12,2,256]{3,2,1,0:T(2,128)S(1)}, u32[]{:S(2)}, u32[]{:S(2)}) %collective-permute-start.16) | collective-permute-done | bytes 294944 | tf_op jit(solution)/shard_map/ppermute | solution.py:17
  72.1 1.5 %collective-permute-done.17 = f32[12,12,2,256]{3,2,1,0:T(2,128)S(1)} collective-permute-done((f32[12,12,2,256]{3,2,1,0:T(2,128)S(1)}, f32[12,12,2,256]{3,2,1,0:T(2,128)S(1)}, u32[]{:S(2)}, u32[]{:S(2)}) %collective-permute-start.17) | collective-permute-done | bytes 294944 | tf_op jit(solution)/shard_map/ppermute | solution.py:18
  73.6 0.7 pad_maximum_fusion
  74.3 0.1 fusion.10
  74.4 0.2 fusion.9
  74.6 0.1 bitcast_dynamic-update-slice_fusion
  74.7 0.0 copy-start.1
  74.7 0.0 copy-start.2
  74.8 0.0 copy-start.3
  74.8 0.0 copy-start.4
  74.8 0.2 fusion.8
  75.0 0.2 fusion.7.ysh_ref
  75.1 2.5 %copy-done.5 = f32[5,12,12,8,256]{4,3,2,1,0:T(8,128)} copy-done((f32[5,12,12,8,256]{4,3,2,1,0:T(8,128)}, f32[5,12,12,8,256]{4,3,2,1,0:T(8,128)S(1)}, u32[]{:S(2)}) %copy-start.5) | copy-done | bytes 5898264
  77.7 22.1 %shard_map.113 = bf16[512,256]{1,0:T(8,128)(2,1)} custom-call(s32[294]{0:T(512)S(1)} %copy-done.4, f32[5,12,12,8,256]{4,3,2,1,0:T(8,128)} %copy-done.5, f32[512,98]{1,0:T(8,128)S(1)} %bitcast.33, f32[98,256]{1,0:T(8,128)S(1)} %copy-done.2, f32[98,256]{1,0:T(8,128)S(1)} %copy-done.3, bf16[256,256]{1,0:T(8,128)(2,1)S(1)} %copy-done.1, f32[1,256]{1,0:T(1,128)S(1)} %fusion.17), custom_call_target="tpu_custom_call" | custom-call | tf_op jit(solution)/shard_map/pallas_call | solution.py:85
  99.8 0.9 fusion.16
  100.7 0.8 collective-permute-start.18
  101.4 4.9 %collective-permute-start.19 = (bf16[2,8,8,256]{3,2,1,0:T(8,128)(2,1)S(1)}, bf16[2,8,8,256]{3,2,1,0:T(8,128)(2,1)S(1)}, u32[]{:S(2)}, u32[]{:S(2)}) collective-permute-start(bf16[2,8,8,256]{3,2,1,0:T(8,128)(2,1)S(1)} %bitcast.41), channel_id=1, source_target_pairs={{16,0},{32,16},{48,32},{64,48},{80,64},{96,80},{112,96},{128,112},... | collective-permute-start | bytes 196616 | tf_op jit(solution)/shard_map/ppermute | solution.py:18
  106.4 2.2 %collective-permute-done.18 = bf16[2,8,8,256]{3,2,1,0:T(8,128)(2,1)S(1)} collective-permute-done((bf16[2,8,8,256]{3,2,1,0:T(8,128)(2,1)S(1)}, bf16[2,8,8,256]{3,2,1,0:T(8,128)(2,1)S(1)}, u32[]{:S(2)}, u32[]{:S(2)}) %collective-permute-start.18) | collective-permute-done | bytes 65568 | tf_op jit(solution)/shard_map/ppermute | solution.py:17
  108.6 0.0 collective-permute-done.19
  108.6 1.0 pad_maximum_fusion.2
  109.6 4.3 %fusion.6 = f32[4096]{0:T(1024)} fusion(bf16[768,256]{1,0:T(8,128)(2,1)S(1)} %bitcast.39, s32[4096]{0:T(1024)S(1)} %copy-done.9, bf16[4096,256]{0,1:T(8,128)(2,1)S(1)} %copy.12), kind=kOutput, calls=%fused_computation.12 | convolution fusion | flops 1616900096 | bytes 2523136 | tf_op jit(solution)/shard_map/dot_general | solution.py:126
  (22 shorter events, 0.2 us)
Async XLA Ops:
  0.6 38.3 %copy-start = (f32[256,256]{1,0:T(8,128)S(1)}, f32[256,256]{1,0:T(8,128)}, u32[]{:S(2)}) copy-start(f32[256,256]{1,0:T(8,128)} %param.22) | copy-start | bytes 786436
  0.6 3.0 %copy-start.7 = (f32[4096]{0:T(1024)S(1)}, f32[4096]{0:T(1024)}, u32[]{:S(2)}) copy-start(f32[4096]{0:T(1024)} %param.15) | copy-start | bytes 49156
  0.7 3.0 %copy-start.8 = (s32[4096]{0:T(1024)S(1)}, s32[4096]{0:T(1024)}, u32[]{:S(2)}) copy-start(s32[4096]{0:T(1024)} %param.16) | copy-start | bytes 49156
  3.6 35.5 %copy-start.9 = (s32[4096]{0:T(1024)S(1)}, s32[4096]{0:T(1024)}, u32[]{:S(2)}) copy-start(s32[4096]{0:T(1024)} %param.17) | copy-start | bytes 49156
  4.4 3.7 %collective-permute-start = (f32[256]{0:T(256)S(1)}, f32[256]{0:T(256)S(1)}, u32[]{:S(2)}, u32[]{:S(2)}) collective-permute-start(f32[256]{0:T(256)S(1)} %get-tuple-element.30), channel_id=1, source_target_pairs={{0,1},{1,2},{2,3},{3,0},{4,5},{5,6},{6,7},{7,4},{8,9},{9,10},{10,1... | collective-permute-start | bytes 3080 | tf_op jit(solution)/shard_map/ppermute | solution.py:45
  6.7 5.1 %collective-permute-start.1 = (f32[256]{0:T(256)S(1)}, f32[256]{0:T(256)S(1)}, u32[]{:S(2)}, u32[]{:S(2)}) collective-permute-start(f32[256]{0:T(256)S(1)} %get-tuple-element.30), channel_id=1, source_target_pairs={{0,2},{1,3},{2,0},{3,1},{4,6},{5,7},{6,4},{7,5},{8,10},{9,11},{10,... | collective-permute-start | bytes 3080 | tf_op jit(solution)/shard_map/ppermute | solution.py:45
  7.4 4.8 %collective-permute-start.2 = (f32[256]{0:T(256)S(1)}, f32[256]{0:T(256)S(1)}, u32[]{:S(2)}, u32[]{:S(2)}) collective-permute-start(f32[256]{0:T(256)S(1)} %get-tuple-element.30), channel_id=1, source_target_pairs={{0,3},{1,0},{2,1},{3,2},{4,7},{5,4},{6,5},{7,6},{8,11},{9,8},{10,9... | collective-permute-start | bytes 3080 | tf_op jit(solution)/shard_map/ppermute | solution.py:45
  12.2 3.0 %collective-permute-start.3 = (f32[256]{0:T(256)S(1)}, f32[256]{0:T(256)S(1)}, u32[]{:S(2)}, u32[]{:S(2)}) collective-permute-start(f32[256]{0:T(256)S(1)} %add_add_fusion.3), channel_id=1, source_target_pairs={{0,4},{4,8},{8,12},{12,0},{1,5},{5,9},{9,13},{13,1},{2,6},{6,10},{... | collective-permute-start | bytes 3080 | tf_op jit(solution)/shard_map/ppermute | solution.py:45
  12.2 3.7 %collective-permute-start.4 = (f32[256]{0:T(256)S(1)}, f32[256]{0:T(256)S(1)}, u32[]{:S(2)}, u32[]{:S(2)}) collective-permute-start(f32[256]{0:T(256)S(1)} %add_add_fusion.3), channel_id=1, source_target_pairs={{0,8},{4,12},{8,0},{12,4},{1,9},{5,13},{9,1},{13,5},{2,10},{6,14},... | collective-permute-start | bytes 3080 | tf_op jit(solution)/shard_map/ppermute | solution.py:45
  13.8 2.7 %collective-permute-start.5 = (f32[256]{0:T(256)S(1)}, f32[256]{0:T(256)S(1)}, u32[]{:S(2)}, u32[]{:S(2)}) collective-permute-start(f32[256]{0:T(256)S(1)} %add_add_fusion.3), channel_id=1, source_target_pairs={{0,12},{4,0},{8,4},{12,8},{1,13},{5,1},{9,5},{13,9},{2,14},{6,2},{... | collective-permute-start | bytes 3080 | tf_op jit(solution)/shard_map/ppermute | solution.py:45
  16.5 6.4 %collective-permute-start.6 = (f32[256]{0:T(256)S(1)}, f32[256]{0:T(256)S(1)}, u32[]{:S(2)}, u32[]{:S(2)}) collective-permute-start(f32[256]{0:T(256)S(1)} %add_add_fusion.2), channel_id=1, source_target_pairs={{0,16},{16,32},{32,48},{48,0},{64,80},{80,96},{96,112},{112,64},{1... | collective-permute-start | bytes 3080 | tf_op jit(solution)/shard_map/ppermute | solution.py:45
  19.4 3.6 %collective-permute-start.7 = (f32[256]{0:T(256)S(1)}, f32[256]{0:T(256)S(1)}, u32[]{:S(2)}, u32[]{:S(2)}) collective-permute-start(f32[256]{0:T(256)S(1)} %add_add_fusion.2), channel_id=1, source_target_pairs={{0,32},{16,48},{32,0},{48,16},{64,96},{80,112},{96,64},{112,80},{1... | collective-permute-start | bytes 3080 | tf_op jit(solution)/shard_map/ppermute | solution.py:45
  21.3 5.1 %collective-permute-start.8 = (f32[256]{0:T(256)S(1)}, f32[256]{0:T(256)S(1)}, u32[]{:S(2)}, u32[]{:S(2)}) collective-permute-start(f32[256]{0:T(256)S(1)} %add_add_fusion.2), channel_id=1, source_target_pairs={{0,48},{16,0},{32,16},{48,32},{64,112},{80,64},{96,80},{112,96},{1... | collective-permute-start | bytes 3080 | tf_op jit(solution)/shard_map/ppermute | solution.py:45
  26.4 9.2 %collective-permute-start.10 = (f32[256]{0:T(256)S(1)}, f32[256]{0:T(256)S(1)}, u32[]{:S(2)}, u32[]{:S(2)}) collective-permute-start(f32[256]{0:T(256)S(1)} %add_add_fusion.1), channel_id=1, source_target_pairs={{0,128},{16,144},{32,160},{48,176},{64,192},{80,208},{96,224},{112... | collective-permute-start | bytes 3080 | tf_op jit(solution)/shard_map/ppermute | solution.py:45
  32.7 4.5 %collective-permute-start.11 = (f32[256]{0:T(256)S(1)}, f32[256]{0:T(256)S(1)}, u32[]{:S(2)}, u32[]{:S(2)}) collective-permute-start(f32[256]{0:T(256)S(1)} %add_add_fusion.1), channel_id=1, source_target_pairs={{0,192},{16,208},{32,224},{48,240},{64,0},{80,16},{96,32},{112,48}... | collective-permute-start | bytes 3080 | tf_op jit(solution)/shard_map/ppermute | solution.py:45
  33.3 5.7 %collective-permute-start.9 = (f32[256]{0:T(256)S(1)}, f32[256]{0:T(256)S(1)}, u32[]{:S(2)}, u32[]{:S(2)}) collective-permute-start(f32[256]{0:T(256)S(1)} %add_add_fusion.1), channel_id=1, source_target_pairs={{0,64},{16,80},{32,96},{48,112},{64,128},{80,144},{96,160},{112,17... | collective-permute-start | bytes 3080 | tf_op jit(solution)/shard_map/ppermute | solution.py:45
  41.5 10.5 %collective-permute-start.12 = (f32[4,8,8,256]{3,2,1,0:T(8,128)S(1)}, f32[4,8,8,256]{3,2,1,0:T(8,128)S(1)}, u32[]{:S(2)}, u32[]{:S(2)}) collective-permute-start(f32[4,8,8,256]{3,2,1,0:T(8,128)S(1)} %bitcast.40), channel_id=1, source_target_pairs={{0,16},{16,32},{32,48},{48,64},{64,80},{80,96},{96,112},{112,128},... | collective-permute-start | bytes 786440 | tf_op jit(solution)/shard_map/ppermute | solution.py:115
  43.2 12.4 %collective-permute-start.13 = (f32[4,8,8,256]{3,2,1,0:T(8,128)S(1)}, f32[4,8,8,256]{3,2,1,0:T(8,128)S(1)}, u32[]{:S(2)}, u32[]{:S(2)}) collective-permute-start(f32[4,8,8,256]{3,2,1,0:T(8,128)S(1)} %bitcast.37), channel_id=1, source_target_pairs={{16,0},{32,16},{48,32},{64,48},{80,64},{96,80},{112,96},{128,112},... | collective-permute-start | bytes 786440 | tf_op jit(solution)/shard_map/ppermute | solution.py:116
  55.7 8.8 %copy-start.6 = (s32[8,8,8,98]{3,2,1,0:T(8,128)S(1)}, s32[8,8,8,98]{3,2,1,0:T(8,128)}, u32[]{:S(2)}) copy-start(s32[8,8,8,98]{3,2,1,0:T(8,128)} %param.18) | copy-start | bytes 602116
  55.7 5.4 %collective-permute-start.14 = (f32[12,2,8,256]{3,2,1,0:T(8,128)S(1)}, f32[12,2,8,256]{3,2,1,0:T(8,128)S(1)}, u32[]{:S(2)}, u32[]{:S(2)}) collective-permute-start(f32[12,2,8,256]{3,2,1,0:T(8,128)S(1)} %get-tuple-element.36), channel_id=1, source_target_pairs={{0,4},{4,8},{8,12},{12,0},{1,5},{5,9},{9,13},{13,1},{2,6},{6,10},{... | collective-permute-start | bytes 589832 | tf_op jit(solution)/shard_map/ppermute | solution.py:17
  55.8 6.3 %collective-permute-start.15 = (f32[12,2,8,256]{3,2,1,0:T(8,128)S(1)}, f32[12,2,8,256]{3,2,1,0:T(8,128)S(1)}, u32[]{:S(2)}, u32[]{:S(2)}) collective-permute-start(f32[12,2,8,256]{3,2,1,0:T(8,128)S(1)} %get-tuple-element.37), channel_id=1, source_target_pairs={{4,0},{8,4},{12,8},{0,12},{5,1},{9,5},{13,9},{1,13},{6,2},{10,6},{... | collective-permute-start | bytes 589832 | tf_op jit(solution)/shard_map/ppermute | solution.py:18
  62.4 9.7 %collective-permute-start.16 = (f32[12,12,2,256]{3,2,1,0:T(2,128)S(1)}, f32[12,12,2,256]{3,2,1,0:T(2,128)S(1)}, u32[]{:S(2)}, u32[]{:S(2)}) collective-permute-start(f32[12,12,2,256]{3,2,1,0:T(2,128)S(1)} %get-tuple-element.35), channel_id=1, source_target_pairs={{0,1},{1,2},{2,3},{3,0},{4,5},{5,6},{6,7},{7,4},{8,9},{9,10},{10,1... | collective-permute-start | bytes 884744 | tf_op jit(solution)/shard_map/ppermute | solution.py:17
  63.1 10.6 %collective-permute-start.17 = (f32[12,12,2,256]{3,2,1,0:T(2,128)S(1)}, f32[12,12,2,256]{3,2,1,0:T(2,128)S(1)}, u32[]{:S(2)}, u32[]{:S(2)}) collective-permute-start(f32[12,12,2,256]{3,2,1,0:T(2,128)S(1)} %get-tuple-element.34), channel_id=1, source_target_pairs={{1,0},{2,1},{3,2},{0,3},{5,4},{6,5},{7,6},{4,7},{9,8},{10,9},{11,1... | collective-permute-start | bytes 884744 | tf_op jit(solution)/shard_map/ppermute | solution.py:18
  74.7 3.0 %copy-start.1 = (bf16[256,256]{1,0:T(8,128)(2,1)S(1)}, bf16[256,256]{1,0:T(8,128)(2,1)}, u32[]{:S(2)}) copy-start(bf16[256,256]{1,0:T(8,128)(2,1)} %base_ref.1) | copy-start | bytes 393220
  74.7 2.9 %copy-start.2 = (f32[98,256]{1,0:T(8,128)S(1)}, f32[98,256]{1,0:T(8,128)}, u32[]{:S(2)}) copy-start(f32[98,256]{1,0:T(8,128)} %rs_ref.1) | copy-start | bytes 301060
  74.8 2.9 %copy-start.3 = (f32[98,256]{1,0:T(8,128)S(1)}, f32[98,256]{1,0:T(8,128)}, u32[]{:S(2)}) copy-start(f32[98,256]{1,0:T(8,128)} %cs_ref.1) | copy-start | bytes 301060
  74.8 2.9 %copy-start.4 = (s32[294]{0:T(512)S(1)}, s32[294]{0:T(512)}, u32[]{:S(2)}) copy-start(s32[294]{0:T(512)} %constant.59.clone.tab_ref) | copy-start | bytes 3532
  75.1 2.5 %copy-start.5 = (f32[5,12,12,8,256]{4,3,2,1,0:T(8,128)}, f32[5,12,12,8,256]{4,3,2,1,0:T(8,128)S(1)}, u32[]{:S(2)}) copy-start(f32[5,12,12,8,256]{4,3,2,1,0:T(8,128)S(1)} %fusion.7.ysh_ref) | copy-start | bytes 17694724
  100.7 8.0 %collective-permute-start.18 = (bf16[2,8,8,256]{3,2,1,0:T(8,128)(2,1)S(1)}, bf16[2,8,8,256]{3,2,1,0:T(8,128)(2,1)S(1)}, u32[]{:S(2)}, u32[]{:S(2)}) collective-permute-start(bf16[2,8,8,256]{3,2,1,0:T(8,128)(2,1)S(1)} %bitcast.42), channel_id=1, source_target_pairs={{0,16},{16,32},{32,48},{48,64},{64,80},{80,96},{96,112},{112,128},... | collective-permute-start | bytes 196616 | tf_op jit(solution)/shard_map/ppermute | solution.py:17
  101.4 7.2 %collective-permute-start.19 = (bf16[2,8,8,256]{3,2,1,0:T(8,128)(2,1)S(1)}, bf16[2,8,8,256]{3,2,1,0:T(8,128)(2,1)S(1)}, u32[]{:S(2)}, u32[]{:S(2)}) collective-permute-start(bf16[2,8,8,256]{3,2,1,0:T(8,128)(2,1)S(1)} %bitcast.41), channel_id=1, source_target_pairs={{16,0},{32,16},{48,32},{64,48},{80,64},{96,80},{112,96},{128,112},... | collective-permute-start | bytes 196616 | tf_op jit(solution)/shard_map/ppermute | solution.py:18
